TPU v7x, 32 devices: a whole 2x2x4 slice. The times are simulated.
32 devices in a mesh: grp: 2 (over x), date: 16 (over z, y, core).
Axes of the slice: x: 2, y: 2, z: 4, core: 2. Of those that a mesh axis runs over, the one named last changes fastest.
Arguments:
- slc: bfloat16 [16, 2, 128, 2048], P('date', None, 'grp'), parts along dimension 2, may hold values from -6 to 6
- pairs: int32 [64, 2], replicated, may hold values from 0 to 15, as said below
- inverse: bfloat16 [15, 64], replicated, may hold values from -6 to 6
Outputs:
- series: float32 [15, 32, 128], P(None, ('grp', 'date')), parts along dimension 1
There are 2 independent parts, one for each index of `grp`. A program takes and returns all parts, laid end to end along the dimension named above; an argument that names none is the same for every part. Nothing has to cross between parts.
Inputs may be any that keep to these rules, and one draw needn't show every extreme that they name: pairs[p,0] < pairs[p,1] for every pair.
All inputs are finite; a program needn't handle non-finite values.
Results may differ from a plain program's by a relative error of at most 0.0003.
Values may be sent and summed in bfloat16 or wider, within the bound.
No kernel may reach another device: no remote copies, remote signals or barrier semaphores. Data moves between devices by JAX's collectives and lax.ppermute only.
A program may use at most 128 MiB of HBM per device.

v0:
```python
import jax
import jax.numpy as jnp
from jax import lax
from jax.sharding import PartitionSpec as P

LOOK_R = 4
LOOK_C = 16


def coherence(first, second):
    first = first.astype(jnp.float32)
    second = second.astype(jnp.float32)
    cross = first[:, 1] * second[:, 0] - first[:, 0] * second[:, 1]
    power_ref = first[:, 0] * first[:, 0] + first[:, 1] * first[:, 1]
    power_sec = second[:, 0] * second[:, 0] + second[:, 1] * second[:, 1]
    stacked = jnp.stack([cross, power_ref, power_sec])
    three, count, rows, cols = stacked.shape
    rowsum = stacked.reshape(three, count, rows // LOOK_R, LOOK_R, cols).sum(axis=3)
    window = (jnp.arange(cols)[:, None] // LOOK_C == jnp.arange(cols // LOOK_C)[None, :]).astype(
        jnp.float32
    )
    looked = jnp.dot(rowsum, window, precision=lax.Precision.HIGHEST)
    return looked[0] / jnp.sqrt(looked[1] * looked[2] + 1e-06)


def invert(inverse, proxy):
    return jnp.einsum(
        "sp,pxy->sxy", inverse.astype(jnp.float32), proxy, precision=lax.Precision.HIGHEST
    )


def per_device(slc, pairs, inverse):
    stripes = lax.all_to_all(slc, "date", split_axis=2, concat_axis=0, tiled=True)
    first = jnp.take(stripes, pairs[:, 0], axis=0)
    second = jnp.take(stripes, pairs[:, 1], axis=0)
    proxy = coherence(first, second)
    return invert(inverse, proxy)


def solution(mesh):
    in_specs = (P("date", None, "grp", None), P(), P())
    out_specs = P(None, ("grp", "date"), None)
    return jax.shard_map(
        per_device, mesh=mesh, in_specs=in_specs, out_specs=out_specs, check_vma=False
    )
```

profile of v0, /device:TPU:0, one launch (start us, length us, event | category | flops | bytes accessed | tf_op | source)
XLA Modules:
  0.0 41.9 jit_solution(5127418015980830979)
XLA Ops:
  0.0 0.0 copy-start
  0.0 0.0 copy-start.1
  0.0 2.4 %copy.26 = bf16[1,2,64,2048]{3,1,0,2:T(2,128)(2,1)} copy(bf16[1,2,64,2048]{3,2,1,0:T(8,128)(2,1)} %param.5) | data formatting | bytes 1048576 | tf_op args[0]
  2.4 7.4 %all-to-all-start = ((bf16[1,2,64,2048]{3,1,0,2:T(2,128)(2,1)}), bf16[1,2,64,2048]{3,1,0,2:T(2,128)(2,1)S(1)}, u32[]{:S(2)}, u32[]{:S(2)}) async-start(bf16[1,2,64,2048]{3,1,0,2:T(2,128)(2,1)} %copy.26), calls=%async_computation | async-start | bytes 1048576 | tf_op jit(solution)/shard_map/all_to_all | solution.py:33
  9.8 0.0 copy-done.1
  9.9 14.2 %all-to-all-done = bf16[1,2,64,2048]{3,1,0,2:T(2,128)(2,1)S(1)} async-done(((bf16[1,2,64,2048]{3,1,0,2:T(2,128)(2,1)}), bf16[1,2,64,2048]{3,1,0,2:T(2,128)(2,1)S(1)}, u32[]{:S(2)}, u32[]{:S(2)}) %all-to-all-start) | async-done | bytes 524320 | tf_op jit(solution)/shard_map/all_to_all | solution.py:33
  24.1 0.3 copy.38
  24.4 2.4 %gather_fusion = bf16[64,2,4,2048]{3,2,1,0:T(4,128)(2,1)S(1)} fusion(bf16[16,2,4,2048]{3,2,1,0:T(4,128)(2,1)S(1)} %bitcast.30, s32[1024]{0:T(1024)S(1)} %pad_clamp_fusion.1), kind=kCustom, calls=%fused_computation.clone | custom fusion | bytes 4194560 | tf_op jit(solution)/shard_map/jit(_take)/gather | solution.py:34
  26.7 3.6 %gather_fusion.1 = bf16[64,2,4,2048]{3,2,1,0:T(4,128)(2,1)} fusion(bf16[16,2,4,2048]{3,2,1,0:T(4,128)(2,1)S(1)} %bitcast.31, s32[1024]{0:T(1024)S(1)} %pad_clamp_fusion), kind=kCustom, calls=%fused_computation.1.clone | custom fusion | bytes 4194560 | tf_op jit(solution)/shard_map/jit(_take)/gather | solution.py:35
  30.3 7.5 %fusion = (f32[64,2,4,2048]{3,0,2,1:T(8,128)S(1)}, f32[64,2,4,2048]{3,0,2,1:T(8,128)S(1)}) fusion(bf16[64,2,4,2048]{3,2,1,0:T(4,128)(2,1)} %gather_fusion.1, pred[64]{0:T(512)(128)(4,1)S(1)} %get-tuple-element.13, bf16[64,2,4,2048]{3,2,1,0:T(4,128)(2,1)S(1)} %gather_fusion, pred[64]{0:T(512)(128)(4,1)S(1)} %get-tuple-element.6), kind=kLoop, calls=%fused_computation.4 | loop fusion | flops 4194304 | bytes 12583040 | tf_op jit(solution)/shard_map/convert_element_type | solution.py:12
  37.8 1.6 %subtract_bitcast_fusion = (f32[1,64,4,2048]{3,1,2,0:T(8,128)S(1)}, f32[1,64,4,2048]{3,1,2,0:T(8,128)S(1)}, f32[1,64,4,2048]{3,1,2,0:T(8,128)S(1)}) fusion(f32[64,2,4,2048]{3,0,2,1:T(8,128)S(1)} %get-tuple-element.15, f32[64,2,4,2048]{3,0,2,1:T(8,128)S(1)} %get-tuple-element.16), kind=kLoop, calls=%fused_computation.9 | loop fusion | flops 4718592 | bytes 14680064 | tf_op jit(solution)/shard_map/sub | solution.py:13
  39.5 0.7 %maximum_reduce_fusion = f32[3,64,2048]{2,1,0:T(8,128)S(1)} fusion(f32[1,64,4,2048]{3,1,2,0:T(8,128)S(1)} %get-tuple-element.12, f32[1,64,4,2048]{3,1,2,0:T(8,128)S(1)} %get-tuple-element.11, f32[1,64,4,2048]{3,1,2,0:T(8,128)S(1)} %get-tuple-element.10), kind=kLoop, calls=%fused_computation.2 | loop fusion | flops 4325376 | bytes 7864320 | tf_op jit(solution)/shard_map/reduce_sum | solution.py:18
  40.1 1.0 %fusion.3 = f32[3,64,128]{2,1,0:T(8,128)S(1)} fusion(f32[3,64,2048]{2,1,0:T(8,128)S(1)} %maximum_reduce_fusion, s32[2048]{0:T(1024)S(1)} %add_select_fusion), kind=kOutput, calls=%fused_computation.13 | convolution fusion | flops 604241920 | bytes 1679360 | tf_op jit(solution)/shard_map/dot_general | solution.py:22
  41.2 0.0 copy-done
  41.2 0.1 convolution_bitcast_fusion
  41.3 0.6 %copy.30 = f32[15,1,128]{2,1,0:T(1,128)} copy(f32[15,1,128]{2,0,1:T(8,128)S(1)} %convolution_bitcast_fusion) | data formatting | bytes 15360 | tf_op jit(solution)/shard_map/sp,pxy->sxy/dot_general | solution.py:27
  (4 shorter events, 0.0 us)
Async XLA Ops:
  0.0 41.2 %copy-start = (bf16[15,64]{1,0:T(8,128)(2,1)S(1)}, bf16[15,64]{1,0:T(8,128)(2,1)}, u32[]{:S(2)}) copy-start(bf16[15,64]{1,0:T(8,128)(2,1)} %param.7) | copy-start | bytes 5764
  0.0 9.8 %copy-start.1 = (s32[64,2]{0,1:T(2,128)S(1)}, s32[64,2]{0,1:T(2,128)}, u32[]{:S(2)}) copy-start(s32[64,2]{0,1:T(2,128)} %param.6) | copy-start | bytes 1540
  2.4 21.7 %all-to-all-start = ((bf16[1,2,64,2048]{3,1,0,2:T(2,128)(2,1)}), bf16[1,2,64,2048]{3,1,0,2:T(2,128)(2,1)S(1)}, u32[]{:S(2)}, u32[]{:S(2)}) async-start(bf16[1,2,64,2048]{3,1,0,2:T(2,128)(2,1)} %copy.26), calls=%async_computation | async-start | bytes 1048576 | tf_op jit(solution)/shard_map/all_to_all | solution.py:33
where the time goes:
time: 42.2 us; the launch traced here: 41.9 us
  waiting for transfers between devices  14.2 us (34%)
  other arithmetic  9.83 us (23%)
  local copies, waits for them, and re-layouts  9.23 us (22%)
  starting transfers between devices  7.41 us (18%)
  matrix products  1.16 us (3%)
    all_to_all x1, waiting for transfers between devices, per_device(): lax.all_to_all(slc, 'date', split_axis=2, concat_axis=0, tiled=True)  14.2 us
    convert_element_type x1, other arithmetic, coherence(): second = second.astype(jnp.float32)  7.53 us
    all_to_all x1, starting transfers between devices, per_device(): lax.all_to_all(slc, 'date', split_axis=2, concat_axis=0, tiled=True)  7.41 us
    gather x1, local copies, waits for them, and re-layouts, per_device(): second = jnp.take(stripes, pairs[:, 1], axis=0)  3.56 us
    unnamed x5, local copies, waits for them, and re-layouts  2.41 us
    gather x1, local copies, waits for them, and re-layouts, per_device(): first = jnp.take(stripes, pairs[:, 0], axis=0)  2.36 us
    sub x1, other arithmetic, coherence(): cross = first[:, 1] * second[:, 0] - first[:, 0] * second[:, 1]  1.62 us
    dot_general x1, matrix products, coherence(): looked = jnp.dot(rowsum, window, precision=lax.Precision.HIGHEST)  1.03 us
  transfers between devices with their start and end apart: 1, of which 1 were waited for; matrix products, arithmetic and copies ran while one was open for 0% of the time, Pallas kernels for 0%

commit v1 on v0

v1 whole, which is shorter than its diff:
```python
import functools

import jax
import jax.numpy as jnp
from jax import lax
from jax.experimental import pallas as pl
from jax.experimental.pallas import tpu as pltpu
from jax.sharding import PartitionSpec as P

LOOK_R = 4
LOOK_C = 16


def split3(x):
    hi = x.astype(jnp.bfloat16)
    rest = x - hi.astype(jnp.float32)
    mid = rest.astype(jnp.bfloat16)
    lo = (rest - mid.astype(jnp.float32)).astype(jnp.bfloat16)
    return hi, mid, lo


def dot3(parts, w, lhs_is_split):
    out = None
    for part in parts:
        if lhs_is_split:
            term = jnp.dot(part, w, preferred_element_type=jnp.float32)
        else:
            term = jnp.dot(w, part, preferred_element_type=jnp.float32)
        out = term if out is None else out + term
    return out


def kernel(n_date, n_pair, pairs_s, pairs_v, st_ref, inv_ref, out_ref, f_ref, rows_ref):
    cols = st_ref.shape[-1]
    looks = cols // LOOK_C

    def date_body(g, carry):
        acc = jnp.zeros((8, cols), jnp.float32)
        sub = lax.broadcasted_iota(jnp.int32, (8, cols), 0)
        for i in range(8):
            d = g * 8 + i
            re = st_ref[d, 0].astype(jnp.float32)
            im = st_ref[d, 1].astype(jnp.float32)
            f_ref[d, 0:LOOK_R, :] = re
            f_ref[d, LOOK_R:2 * LOOK_R, :] = im
            row = jnp.sum(re * re + im * im, axis=0, keepdims=True)
            acc = jnp.where(sub == i, jnp.broadcast_to(row, (8, cols)), acc)
        start = pl.multiple_of(n_pair + g * 8, 8)
        rows_ref[pl.ds(start, 8), :] = acc
        return carry

    lax.fori_loop(0, n_date // 8, date_body, 0)

    def pair_body(g, carry):
        acc = jnp.zeros((8, cols), jnp.float32)
        sub = lax.broadcasted_iota(jnp.int32, (8, cols), 0)
        for i in range(8):
            p = g * 8 + i
            a = pairs_s[2 * p]
            b = pairs_s[2 * p + 1]
            a0 = f_ref[a, 0:LOOK_R, :]
            a1 = f_ref[a, LOOK_R:2 * LOOK_R, :]
            b0 = f_ref[b, 0:LOOK_R, :]
            b1 = f_ref[b, LOOK_R:2 * LOOK_R, :]
            cross = a1 * b0 - a0 * b1
            row = jnp.sum(cross, axis=0, keepdims=True)
            acc = jnp.where(sub == i, jnp.broadcast_to(row, (8, cols)), acc)
        start = pl.multiple_of(g * 8, 8)
        rows_ref[pl.ds(start, 8), :] = acc
        return carry

    lax.fori_loop(0, n_pair // 8, pair_body, 0)

    c_idx = lax.broadcasted_iota(jnp.int32, (cols, looks), 0)
    j_idx = lax.broadcasted_iota(jnp.int32, (cols, looks), 1)
    window = ((c_idx >= j_idx * LOOK_C) & (c_idx < j_idx * LOOK_C + LOOK_C)).astype(jnp.bfloat16)
    looked = dot3(split3(rows_ref[...]), window, True)
    looked_cross = looked[0:n_pair]
    looked_pow = looked[n_pair:n_pair + n_date]

    date_idx = lax.broadcasted_iota(jnp.int32, (n_pair, n_date), 1)
    sel_a = (pairs_v[:, 0:1] == date_idx).astype(jnp.bfloat16)
    sel_b = (pairs_v[:, 1:2] == date_idx).astype(jnp.bfloat16)
    pow_parts = split3(looked_pow)
    looked_ref = dot3(pow_parts, sel_a, False)
    looked_sec = dot3(pow_parts, sel_b, False)

    proxy = looked_cross / jnp.sqrt(looked_ref * looked_sec + 1e-06)
    out_ref[...] = dot3(split3(proxy), inv_ref[...], False)


def per_device(slc, pairs, inverse):
    n_date = lax.axis_size("date")
    n_pair = pairs.shape[0]
    steps = inverse.shape[0]
    stripes = lax.all_to_all(slc, "date", split_axis=2, concat_axis=0, tiled=True)
    _, _, rows, cols = stripes.shape
    assert rows == LOOK_R and n_date % 8 == 0 and n_pair % 8 == 0
    looks = cols // LOOK_C
    out = pl.pallas_call(
        functools.partial(kernel, n_date, n_pair),
        out_shape=jax.ShapeDtypeStruct((steps, looks), jnp.float32),
        in_specs=[
            pl.BlockSpec(memory_space=pltpu.SMEM),
            pl.BlockSpec(memory_space=pltpu.VMEM),
            pl.BlockSpec(memory_space=pltpu.VMEM),
            pl.BlockSpec(memory_space=pltpu.VMEM),
        ],
        out_specs=pl.BlockSpec(memory_space=pltpu.VMEM),
        scratch_shapes=[
            pltpu.VMEM((n_date, 2 * LOOK_R, cols), jnp.float32),
            pltpu.VMEM((n_pair + n_date, cols), jnp.float32),
        ],
    )(pairs.reshape(-1), pairs, stripes, inverse)
    return out.reshape(steps, 1, looks)


def solution(mesh):
    in_specs = (P("date", None, "grp", None), P(), P())
    out_specs = P(None, ("grp", "date"), None)
    return jax.shard_map(
        per_device, mesh=mesh, in_specs=in_specs, out_specs=out_specs, check_vma=False
    )
```

time: 42.2 us -> 32 us (0.76)
  other arithmetic: 9.83 us -> 0 us
  Pallas kernels: 0 us -> 5.15 us
  local copies, waits for them, and re-layouts: 9.23 us -> 5.49 us
  matrix products: 1.16 us -> 0 us
  waiting for transfers between devices: 14.2 us -> 13.5 us
    convert_element_type x1 -> x0, other arithmetic: 7.53 us -> none  [coherence(): second = second.astype(jnp.float32)]
    gather x2 -> x0, local copies, waits for them, and re-layouts: 5.92 us -> none  [the longest x1 3.56 us: per_device(): second = jnp.take(stripes, pairs[:, 1], axis=0)]
    pallas_call x0 -> x1, Pallas kernels: none -> 5.15 us  [per_device(): pl.pallas_call(functools.partial(kernel, n_date, n_pair), out_shape=jax.S...]
    reshape x0 -> x2, local copies, waits for them, and re-layouts: none -> 1.95 us  [the longest x1 1.3 us: per_device(): return out.reshape(steps, 1, looks)]
    sub x1 -> x0, other arithmetic: 1.62 us -> none  [coherence(): cross = first[:, 1] * second[:, 0] - first[:, 0] * second[:, 1]]
    dot_general x2 -> x0, matrix products: 1.16 us -> none  [the longest x1 1.03 us: coherence(): looked = jnp.dot(rowsum, window, precision=lax.Precision.HIGHEST)]
    all_to_all x1, local copies, waits for them, and re-layouts: 0.27 us -> 1.07 us  [per_device(): lax.all_to_all(slc, 'date', split_axis=2, concat_axis=0, tiled=True)]
    all_to_all x1, waiting for transfers between devices: 14.2 us -> 13.5 us  [per_device(): lax.all_to_all(slc, 'date', split_axis=2, concat_axis=0, tiled=True)]
  transfers between devices with their start and end apart: 1 -> 1, of which waited for: 1 -> 1; matrix products, arithmetic and copies ran while one was open for 0% -> 2% of each run, Pallas kernels for 0% -> 0%
where the time goes in v1:
time: 32 us; the launch traced here: 31.7 us
  waiting for transfers between devices  13.5 us (42%)
  starting transfers between devices  7.55 us (24%)
  local copies, waits for them, and re-layouts  5.49 us (17%)
  Pallas kernels  5.15 us (16%)
    all_to_all x1, waiting for transfers between devices, per_device(): lax.all_to_all(slc, 'date', split_axis=2, concat_axis=0, tiled=True)  13.5 us
    all_to_all x1, starting transfers between devices, per_device(): lax.all_to_all(slc, 'date', split_axis=2, concat_axis=0, tiled=True)  7.55 us
    pallas_call x1, Pallas kernels, per_device(): pl.pallas_call(functools.partial(kernel, n_date, n_pair), out_shape=jax.S...  5.15 us
    unnamed x6, local copies, waits for them, and re-layouts  2.47 us
    reshape x1, local copies, waits for them, and re-layouts, per_device(): return out.reshape(steps, 1, looks)  1.3 us
    all_to_all x1, local copies, waits for them, and re-layouts, per_device(): lax.all_to_all(slc, 'date', split_axis=2, concat_axis=0, tiled=True)  1.07 us
    reshape x1, local copies, waits for them, and re-layouts, per_device(): pairs.reshape(-1)  0.65 us
  transfers between devices with their start and end apart: 1, of which 1 were waited for; matrix products, arithmetic and copies ran while one was open for 2% of the time, Pallas kernels for 0%

profile of v1, /device:TPU:0, one launch (start us, length us, event | category | flops | bytes accessed | tf_op | source)
XLA Modules:
  0.0 31.7 jit_solution(14824285380865054198)
XLA Ops:
  0.0 2.4 %copy.13 = bf16[1,2,64,2048]{3,1,0,2:T(2,128)(2,1)} copy(bf16[1,2,64,2048]{3,2,1,0:T(8,128)(2,1)} %param.3) | data formatting | bytes 1048576 | tf_op args[0]
  2.4 0.0 copy-start.1
  2.4 7.5 %all-to-all-start = ((bf16[1,2,64,2048]{3,1,0,2:T(2,128)(2,1)}), bf16[1,2,64,2048]{3,1,0,2:T(2,128)(2,1)S(1)}, u32[]{:S(2)}, u32[]{:S(2)}) async-start(bf16[1,2,64,2048]{3,1,0,2:T(2,128)(2,1)} %copy.13), calls=%async_computation | async-start | bytes 1048576 | tf_op jit(solution)/shard_map/all_to_all | solution.py:96
  9.9 0.0 copy-done.1
  9.9 0.1 copy.12.pairs_v
  10.0 0.0 copy-start
  10.0 0.7 %reshape.6.pairs_s = s32[128]{0:T(128)} reshape(s32[64,2]{1,0:T(8,128)S(1)} %copy.12.pairs_v) | data formatting | bytes 1024 | tf_op jit(solution)/shard_map/reshape | solution.py:114
  10.7 13.5 %all-to-all-done = bf16[1,2,64,2048]{3,1,0,2:T(2,128)(2,1)S(1)} async-done(((bf16[1,2,64,2048]{3,1,0,2:T(2,128)(2,1)}), bf16[1,2,64,2048]{3,1,0,2:T(2,128)(2,1)S(1)}, u32[]{:S(2)}, u32[]{:S(2)}) %all-to-all-start) | async-done | bytes 524320 | tf_op jit(solution)/shard_map/all_to_all | solution.py:96
  24.2 1.1 %copy.18 = bf16[1,2,16,4,2048]{4,3,1,2,0:T(4,128)(2,1)} copy(bf16[1,2,16,4,2048]{4,1,3,2,0:T(2,128)(2,1)S(1)} %bitcast.7) | data formatting | bytes 1048576 | tf_op jit(solution)/shard_map/all_to_all | solution.py:96
  25.3 0.0 copy-done
  25.3 5.1 %shard_map.37 = f32[15,128]{1,0:T(8,128)} custom-call(s32[128]{0:T(128)} %reshape.6.pairs_s, s32[64,2]{1,0:T(8,128)} %copy-done, bf16[16,2,4,2048]{3,2,1,0:T(4,128)(2,1)} %bitcast.8, bf16[15,64]{1,0:T(8,128)(2,1)} %inv_ref.1), custom_call_target="tpu_custom_call" | custom-call | tf_op jit(solution)/shard_map/pallas_call | solution.py:100
  30.4 1.3 %copy.16 = f32[15,1,128]{2,1,0:T(1,128)} copy(f32[15,1,128]{2,0,1:T(8,128)} %bitcast.9) | data formatting | bytes 15360 | tf_op jit(solution)/shard_map/reshape | solution.py:115
Async XLA Ops:
  2.4 7.6 %copy-start.1 = (s32[64,2]{0,1:T(2,128)S(1)}, s32[64,2]{0,1:T(2,128)}, u32[]{:S(2)}) copy-start(s32[64,2]{0,1:T(2,128)} %param.4) | copy-start | bytes 1540
  2.4 21.8 %all-to-all-start = ((bf16[1,2,64,2048]{3,1,0,2:T(2,128)(2,1)}), bf16[1,2,64,2048]{3,1,0,2:T(2,128)(2,1)S(1)}, u32[]{:S(2)}, u32[]{:S(2)}) async-start(bf16[1,2,64,2048]{3,1,0,2:T(2,128)(2,1)} %copy.13), calls=%async_computation | async-start | bytes 1048576 | tf_op jit(solution)/shard_map/all_to_all | solution.py:96
  10.0 15.2 %copy-start = (s32[64,2]{1,0:T(8,128)}, s32[64,2]{1,0:T(8,128)S(1)}, u32[]{:S(2)}) copy-start(s32[64,2]{1,0:T(8,128)S(1)} %copy.12.pairs_v) | copy-start | bytes 1540

commit v2 on v1

--- a/solution.py
+++ b/solution.py
@@ -56,8 +56,8 @@
         sub = lax.broadcasted_iota(jnp.int32, (8, cols), 0)
         for i in range(8):
             p = g * 8 + i
-            a = pairs_s[2 * p]
-            b = pairs_s[2 * p + 1]
+            a = pairs_s[p, 0]
+            b = pairs_s[p, 1]
             a0 = f_ref[a, 0:LOOK_R, :]
             a1 = f_ref[a, LOOK_R:2 * LOOK_R, :]
             b0 = f_ref[b, 0:LOOK_R, :]
@@ -86,7 +86,9 @@
     looked_sec = dot3(pow_parts, sel_b, False)
 
     proxy = looked_cross / jnp.sqrt(looked_ref * looked_sec + 1e-06)
-    out_ref[...] = dot3(split3(proxy), inv_ref[...], False)
+    series = dot3(split3(proxy), inv_ref[...], False)
+    for s in range(series.shape[0]):
+        out_ref[s] = series[s:s + 1, :]
 
 
 def per_device(slc, pairs, inverse):
@@ -99,7 +101,7 @@
     looks = cols // LOOK_C
     out = pl.pallas_call(
         functools.partial(kernel, n_date, n_pair),
-        out_shape=jax.ShapeDtypeStruct((steps, looks), jnp.float32),
+        out_shape=jax.ShapeDtypeStruct((steps, 1, looks), jnp.float32),
         in_specs=[
             pl.BlockSpec(memory_space=pltpu.SMEM),
             pl.BlockSpec(memory_space=pltpu.VMEM),
@@ -111,8 +113,8 @@
             pltpu.VMEM((n_date, 2 * LOOK_R, cols), jnp.float32),
             pltpu.VMEM((n_pair + n_date, cols), jnp.float32),
         ],
-    )(pairs.reshape(-1), pairs, stripes, inverse)
-    return out.reshape(steps, 1, looks)
+    )(pairs, pairs, stripes, inverse)
+    return out
 
 
 def solution(mesh):

time: 32 us -> 31 us (0.969)
  local copies, waits for them, and re-layouts: 5.49 us -> 4.16 us
    reshape x2 -> x0, local copies, waits for them, and re-layouts: 1.95 us -> none  [the longest x1 1.3 us: per_device(): return out.reshape(steps, 1, looks)]
    unnamed x6 -> x4, local copies, waits for them, and re-layouts: 2.47 us -> 3.09 us
where the time goes in v2:
time: 31 us; the launch traced here: 30.7 us
  waiting for transfers between devices  13.5 us (44%)
  starting transfers between devices  7.55 us (24%)
  Pallas kernels  5.43 us (18%)
  local copies, waits for them, and re-layouts  4.16 us (13%)
    all_to_all x1, waiting for transfers between devices, per_device(): lax.all_to_all(slc, 'date', split_axis=2, concat_axis=0, tiled=True)  13.5 us
    all_to_all x1, starting transfers between devices, per_device(): lax.all_to_all(slc, 'date', split_axis=2, concat_axis=0, tiled=True)  7.55 us
    pallas_call x1, Pallas kernels, per_device(): pl.pallas_call(functools.partial(kernel, n_date, n_pair), out_shape=jax.S...  5.43 us
    unnamed x4, local copies, waits for them, and re-layouts  3.09 us
    all_to_all x1, local copies, waits for them, and re-layouts, per_device(): lax.all_to_all(slc, 'date', split_axis=2, concat_axis=0, tiled=True)  1.07 us
  transfers between devices with their start and end apart: 1, of which 1 were waited for; matrix products, arithmetic and copies ran while one was open for 2% of the time, Pallas kernels for 0%

profile of v2, /device:TPU:0, one launch (start us, length us, event | category | flops | bytes accessed | tf_op | source)
XLA Modules:
  0.0 30.7 jit_solution(7430537029836395460)
XLA Ops:
  0.0 2.4 %copy.10 = bf16[1,2,64,2048]{3,1,0,2:T(2,128)(2,1)} copy(bf16[1,2,64,2048]{3,2,1,0:T(8,128)(2,1)} %param.3) | data formatting | bytes 1048576 | tf_op args[0]
  2.4 0.0 copy-start
  2.4 7.5 %all-to-all-start = ((bf16[1,2,64,2048]{3,1,0,2:T(2,128)(2,1)}), bf16[1,2,64,2048]{3,1,0,2:T(2,128)(2,1)S(1)}, u32[]{:S(2)}, u32[]{:S(2)}) async-start(bf16[1,2,64,2048]{3,1,0,2:T(2,128)(2,1)} %copy.10), calls=%async_computation | async-start | bytes 1048576 | tf_op jit(solution)/shard_map/all_to_all | solution.py:98
  9.9 0.0 copy-done
  9.9 0.7 %copy.12.pairs_s.pairs_v = s32[64,2]{1,0:T(8,128)} copy(s32[64,2]{0,1:T(2,128)S(1)} %copy-done) | data formatting | bytes 1024 | tf_op args[1]
  10.7 13.5 %all-to-all-done = bf16[1,2,64,2048]{3,1,0,2:T(2,128)(2,1)S(1)} async-done(((bf16[1,2,64,2048]{3,1,0,2:T(2,128)(2,1)}), bf16[1,2,64,2048]{3,1,0,2:T(2,128)(2,1)S(1)}, u32[]{:S(2)}, u32[]{:S(2)}) %all-to-all-start) | async-done | bytes 524320 | tf_op jit(solution)/shard_map/all_to_all | solution.py:98
  24.2 1.1 %copy.15 = bf16[1,2,16,4,2048]{4,3,1,2,0:T(4,128)(2,1)} copy(bf16[1,2,16,4,2048]{4,1,3,2,0:T(2,128)(2,1)S(1)} %bitcast.6) | data formatting | bytes 1048576 | tf_op jit(solution)/shard_map/all_to_all | solution.py:98
  25.3 5.4 %shard_map.37 = f32[15,1,128]{2,1,0:T(1,128)} custom-call(s32[64,2]{1,0:T(8,128)} %copy.12.pairs_s.pairs_v, s32[64,2]{1,0:T(8,128)} %copy.12.pairs_s.pairs_v, bf16[16,2,4,2048]{3,2,1,0:T(4,128)(2,1)} %bitcast.7, bf16[15,64]{1,0:T(8,128)(2,1)} %inv_ref.1), custom_call_target="tpu_custom_call" | custom-call | tf_op jit(solution)/shard_map/pallas_call | solution.py:102
Async XLA Ops:
  2.4 7.6 %copy-start = (s32[64,2]{0,1:T(2,128)S(1)}, s32[64,2]{0,1:T(2,128)}, u32[]{:S(2)}) copy-start(s32[64,2]{0,1:T(2,128)} %param.4) | copy-start | bytes 1540
  2.4 21.8 %all-to-all-start = ((bf16[1,2,64,2048]{3,1,0,2:T(2,128)(2,1)}), bf16[1,2,64,2048]{3,1,0,2:T(2,128)(2,1)S(1)}, u32[]{:S(2)}, u32[]{:S(2)}) async-start(bf16[1,2,64,2048]{3,1,0,2:T(2,128)(2,1)} %copy.10), calls=%async_computation | async-start | bytes 1048576 | tf_op jit(solution)/shard_map/all_to_all | solution.py:98

commit v3 on v2

--- a/solution.py
+++ b/solution.py
@@ -95,8 +95,10 @@
     n_date = lax.axis_size("date")
     n_pair = pairs.shape[0]
     steps = inverse.shape[0]
-    stripes = lax.all_to_all(slc, "date", split_axis=2, concat_axis=0, tiled=True)
-    _, _, rows, cols = stripes.shape
+    _, _, all_rows, cols = slc.shape
+    rows = all_rows // n_date
+    chunks = slc.reshape(2, n_date, rows, cols).transpose(1, 0, 2, 3)
+    stripes = lax.all_to_all(chunks, "date", split_axis=0, concat_axis=0, tiled=True)
     assert rows == LOOK_R and n_date % 8 == 0 and n_pair % 8 == 0
     looks = cols // LOOK_C
     out = pl.pallas_call(

time: 31 us -> 31 us (level)
    all_to_all x1 -> x0, local copies, waits for them, and re-layouts: 1.07 us -> none  [per_device(): lax.all_to_all(slc, 'date', split_axis=2, concat_axis=0, tiled=True)]
    reshape x0 -> x1, local copies, waits for them, and re-layouts: none -> 1.07 us  [per_device(): chunks = slc.reshape(2, n_date, rows, cols).transpose(1, 0, 2, 3)]
    unnamed x4 -> x6, local copies, waits for them, and re-layouts: 3.09 us -> 3.07 us
where the time goes in v3:
time: 31 us; the launch traced here: 30.7 us
  waiting for transfers between devices  13.6 us (44%)
  starting transfers between devices  7.55 us (24%)
  Pallas kernels  5.43 us (18%)
  local copies, waits for them, and re-layouts  4.14 us (13%)
    all_to_all x1, waiting for transfers between devices, per_device(): lax.all_to_all(chunks, 'date', split_axis=0, concat_axis=0, tiled=True)  13.6 us
    all_to_all x1, starting transfers between devices, per_device(): lax.all_to_all(chunks, 'date', split_axis=0, concat_axis=0, tiled=True)  7.55 us
    pallas_call x1, Pallas kernels, per_device(): pl.pallas_call(functools.partial(kernel, n_date, n_pair), out_shape=jax.S...  5.43 us
    unnamed x6, local copies, waits for them, and re-layouts  3.07 us
    reshape x1, local copies, waits for them, and re-layouts, per_device(): chunks = slc.reshape(2, n_date, rows, cols).transpose(1, 0, 2, 3)  1.07 us
  transfers between devices with their start and end apart: 1, of which 1 were waited for; matrix products, arithmetic and copies ran while one was open for 2% of the time, Pallas kernels for 0%

profile of v3, /device:TPU:0, one launch (start us, length us, event | category | flops | bytes accessed | tf_op | source)
XLA Modules:
  0.0 30.7 jit_solution(138942599508143566)
XLA Ops:
  0.0 1.6 %copy.6 = bf16[1,2,64,2048]{3,1,2,0:T(2,128)(2,1)S(1)} copy(bf16[1,2,64,2048]{3,2,1,0:T(8,128)(2,1)} %param.3) | data formatting | bytes 1048576 | tf_op args[0]
  1.6 1.1 %copy.11 = bf16[2,16,4,2048]{3,2,0,1:T(4,128)(2,1)} copy(bf16[2,16,4,2048]{3,0,2,1:T(2,128)(2,1)S(1)} %bitcast.4) | data formatting | bytes 1048576 | tf_op jit(solution)/shard_map/reshape | solution.py:100
  2.7 0.0 copy-start.1
  2.7 7.5 %all-to-all-start = ((bf16[16,2,4,2048]{3,2,1,0:T(4,128)(2,1)}), bf16[16,2,4,2048]{3,2,1,0:T(4,128)(2,1)S(1)}, u32[]{:S(2)}, u32[]{:S(2)}) async-start(bf16[16,2,4,2048]{3,2,1,0:T(4,128)(2,1)} %bitcast.3), calls=%async_computation | async-start | bytes 1048576 | tf_op jit(solution)/shard_map/all_to_all | solution.py:101
  10.2 0.0 copy-done.1
  10.2 0.7 %copy.8.pairs_s.pairs_v = s32[64,2]{1,0:T(8,128)} copy(s32[64,2]{0,1:T(2,128)S(1)} %copy-done.1) | data formatting | bytes 1024 | tf_op args[1]
  10.9 13.6 %all-to-all-done.st_ref = bf16[16,2,4,2048]{3,2,1,0:T(4,128)(2,1)S(1)} async-done(((bf16[16,2,4,2048]{3,2,1,0:T(4,128)(2,1)}), bf16[16,2,4,2048]{3,2,1,0:T(4,128)(2,1)S(1)}, u32[]{:S(2)}, u32[]{:S(2)}) %all-to-all-start) | async-done | bytes 524320 | tf_op jit(solution)/shard_map/all_to_all | solution.py:101
  24.5 0.0 copy-start
  24.5 0.8 %copy-done = bf16[16,2,4,2048]{3,2,1,0:T(4,128)(2,1)} copy-done((bf16[16,2,4,2048]{3,2,1,0:T(4,128)(2,1)}, bf16[16,2,4,2048]{3,2,1,0:T(4,128)(2,1)S(1)}, u32[]{:S(2)}) %copy-start) | copy-done | bytes 524312
  25.3 5.4 %shard_map.37 = f32[15,1,128]{2,1,0:T(1,128)} custom-call(s32[64,2]{1,0:T(8,128)} %copy.8.pairs_s.pairs_v, s32[64,2]{1,0:T(8,128)} %copy.8.pairs_s.pairs_v, bf16[16,2,4,2048]{3,2,1,0:T(4,128)(2,1)} %copy-done, bf16[15,64]{1,0:T(8,128)(2,1)} %inv_ref.1), custom_call_target="tpu_custom_call" | custom-call | tf_op jit(solution)/shard_map/pallas_call | solution.py:104
Async XLA Ops:
  2.7 7.6 %copy-start.1 = (s32[64,2]{0,1:T(2,128)S(1)}, s32[64,2]{0,1:T(2,128)}, u32[]{:S(2)}) copy-start(s32[64,2]{0,1:T(2,128)} %param.4) | copy-start | bytes 1540
  2.7 21.8 %all-to-all-start = ((bf16[16,2,4,2048]{3,2,1,0:T(4,128)(2,1)}), bf16[16,2,4,2048]{3,2,1,0:T(4,128)(2,1)S(1)}, u32[]{:S(2)}, u32[]{:S(2)}) async-start(bf16[16,2,4,2048]{3,2,1,0:T(4,128)(2,1)} %bitcast.3), calls=%async_computation | async-start | bytes 1048576 | tf_op jit(solution)/shard_map/all_to_all | solution.py:101
  24.5 0.8 %copy-start = (bf16[16,2,4,2048]{3,2,1,0:T(4,128)(2,1)}, bf16[16,2,4,2048]{3,2,1,0:T(4,128)(2,1)S(1)}, u32[]{:S(2)}) copy-start(bf16[16,2,4,2048]{3,2,1,0:T(4,128)(2,1)S(1)} %all-to-all-done.st_ref) | copy-start | bytes 1572868

commit v4 on v3

--- a/solution.py
+++ b/solution.py
@@ -39,11 +39,15 @@
         sub = lax.broadcasted_iota(jnp.int32, (8, cols), 0)
         for i in range(8):
             d = g * 8 + i
-            re = st_ref[d, 0].astype(jnp.float32)
-            im = st_ref[d, 1].astype(jnp.float32)
-            f_ref[d, 0:LOOK_R, :] = re
-            f_ref[d, LOOK_R:2 * LOOK_R, :] = im
-            row = jnp.sum(re * re + im * im, axis=0, keepdims=True)
+            row = None
+            for r in range(LOOK_R):
+                v = st_ref[d * LOOK_R + r].astype(jnp.float32)
+                re = v[0:1]
+                im = v[1:2]
+                f_ref[d, r:r + 1, :] = re
+                f_ref[d, LOOK_R + r:LOOK_R + r + 1, :] = im
+                pw = re * re + im * im
+                row = pw if row is None else row + pw
             acc = jnp.where(sub == i, jnp.broadcast_to(row, (8, cols)), acc)
         start = pl.multiple_of(n_pair + g * 8, 8)
         rows_ref[pl.ds(start, 8), :] = acc
@@ -97,8 +101,8 @@
     steps = inverse.shape[0]
     _, _, all_rows, cols = slc.shape
     rows = all_rows // n_date
-    chunks = slc.reshape(2, n_date, rows, cols).transpose(1, 0, 2, 3)
-    stripes = lax.all_to_all(chunks, "date", split_axis=0, concat_axis=0, tiled=True)
+    got = lax.all_to_all(slc, "date", split_axis=2, concat_axis=2, tiled=True)
+    stripes = got[0].transpose(1, 0, 2)
     assert rows == LOOK_R and n_date % 8 == 0 and n_pair % 8 == 0
     looks = cols // LOOK_C
     out = pl.pallas_call(

time: 31 us -> 30.6 us (0.987)
    reshape x1 -> x0, local copies, waits for them, and re-layouts: 1.07 us -> none  [per_device(): chunks = slc.reshape(2, n_date, rows, cols).transpose(1, 0, 2, 3)]
    unnamed x6, local copies, waits for them, and re-layouts: 3.07 us -> 3.86 us
where the time goes in v4:
time: 30.6 us; the launch traced here: 30.3 us
  waiting for transfers between devices  13.6 us (44%)
  starting transfers between devices  7.55 us (25%)
  Pallas kernels  5.34 us (17%)
  local copies, waits for them, and re-layouts  3.86 us (13%)
    all_to_all x1, waiting for transfers between devices, per_device(): got = lax.all_to_all(slc, 'date', split_axis=2, concat_axis=2, tiled=True)  13.6 us
    all_to_all x1, starting transfers between devices, per_device(): got = lax.all_to_all(slc, 'date', split_axis=2, concat_axis=2, tiled=True)  7.55 us
    pallas_call x1, Pallas kernels, per_device(): pl.pallas_call(functools.partial(kernel, n_date, n_pair), out_shape=jax.S...  5.34 us
    unnamed x6, local copies, waits for them, and re-layouts  3.86 us
  transfers between devices with their start and end apart: 1, of which 1 were waited for; matrix products, arithmetic and copies ran while one was open for 2% of the time, Pallas kernels for 0%

profile of v4, /device:TPU:0, one launch (start us, length us, event | category | flops | bytes accessed | tf_op | source)
XLA Modules:
  0.0 30.3 jit_solution(9783782588829481800)
XLA Ops:
  0.0 2.4 %copy.7 = bf16[1,2,64,2048]{3,1,0,2:T(2,128)(2,1)} copy(bf16[1,2,64,2048]{3,2,1,0:T(8,128)(2,1)} %param.3) | data formatting | bytes 1048576 | tf_op args[0]
  2.4 0.0 copy-start.1
  2.4 7.5 %all-to-all-start = ((bf16[1,2,64,2048]{3,1,0,2:T(2,128)(2,1)}), bf16[1,2,64,2048]{3,1,0,2:T(2,128)(2,1)S(1)}, u32[]{:S(2)}, u32[]{:S(2)}) async-start(bf16[1,2,64,2048]{3,1,0,2:T(2,128)(2,1)} %copy.7), calls=%async_computation | async-start | bytes 1048576 | tf_op jit(solution)/shard_map/all_to_all | solution.py:104
  9.9 0.0 copy-done.1
  9.9 0.7 %copy.8.pairs_s.pairs_v = s32[64,2]{1,0:T(8,128)} copy(s32[64,2]{0,1:T(2,128)S(1)} %copy-done.1) | data formatting | bytes 1024 | tf_op args[1]
  10.6 13.6 %all-to-all-done = bf16[1,2,64,2048]{3,1,0,2:T(2,128)(2,1)S(1)} async-done(((bf16[1,2,64,2048]{3,1,0,2:T(2,128)(2,1)}), bf16[1,2,64,2048]{3,1,0,2:T(2,128)(2,1)S(1)}, u32[]{:S(2)}, u32[]{:S(2)}) %all-to-all-start) | async-done | bytes 524320 | tf_op jit(solution)/shard_map/all_to_all | solution.py:104
  24.2 0.0 copy-start
  24.2 0.8 %copy-done = bf16[1,2,64,2048]{3,1,0,2:T(2,128)(2,1)} copy-done((bf16[1,2,64,2048]{3,1,0,2:T(2,128)(2,1)}, bf16[1,2,64,2048]{3,1,0,2:T(2,128)(2,1)S(1)}, u32[]{:S(2)}) %copy-start) | copy-done | bytes 524312
  25.0 5.3 %shard_map.37 = f32[15,1,128]{2,1,0:T(1,128)} custom-call(s32[64,2]{1,0:T(8,128)} %copy.8.pairs_s.pairs_v, s32[64,2]{1,0:T(8,128)} %copy.8.pairs_s.pairs_v, bf16[64,2,2048]{2,1,0:T(2,128)(2,1)} %bitcast.3, bf16[15,64]{1,0:T(8,128)(2,1)} %inv_ref.1), custom_call_target="tpu_custom_call" | custom-call | tf_op jit(solution)/shard_map/pallas_call | solution.py:108
Async XLA Ops:
  2.4 7.6 %copy-start.1 = (s32[64,2]{0,1:T(2,128)S(1)}, s32[64,2]{0,1:T(2,128)}, u32[]{:S(2)}) copy-start(s32[64,2]{0,1:T(2,128)} %param.4) | copy-start | bytes 1540
  2.4 21.8 %all-to-all-start = ((bf16[1,2,64,2048]{3,1,0,2:T(2,128)(2,1)}), bf16[1,2,64,2048]{3,1,0,2:T(2,128)(2,1)S(1)}, u32[]{:S(2)}, u32[]{:S(2)}) async-start(bf16[1,2,64,2048]{3,1,0,2:T(2,128)(2,1)} %copy.7), calls=%async_computation | async-start | bytes 1048576 | tf_op jit(solution)/shard_map/all_to_all | solution.py:104
  24.2 0.8 %copy-start = (bf16[1,2,64,2048]{3,1,0,2:T(2,128)(2,1)}, bf16[1,2,64,2048]{3,1,0,2:T(2,128)(2,1)S(1)}, u32[]{:S(2)}) copy-start(bf16[1,2,64,2048]{3,1,0,2:T(2,128)(2,1)S(1)} %all-to-all-done) | copy-start | bytes 1572868

commit v5 on v4

--- a/solution.py
+++ b/solution.py
@@ -30,7 +30,7 @@
     return out
 
 
-def kernel(n_date, n_pair, pairs_s, pairs_v, st_ref, inv_ref, out_ref, f_ref, rows_ref):
+def kernel(n_date, n_pair, pairs_s, pairs_v, st_ref, inv_ref, out_ref, f_ref, g_ref, rows_ref):
     cols = st_ref.shape[-1]
     looks = cols // LOOK_C
 
@@ -55,22 +55,35 @@
 
     lax.fori_loop(0, n_date // 8, date_body, 0)
 
+    sub = lax.broadcasted_iota(jnp.int32, (2 * LOOK_R, cols), 0)
+    sign = jnp.where(sub < LOOK_R, -1.0, 1.0).astype(jnp.float32)
+
+    def swap_body(d, carry):
+        g_ref[d] = pltpu.roll(f_ref[d], LOOK_R, 0) * sign
+        return carry
+
+    lax.fori_loop(0, n_date, swap_body, 0)
+
+    masks = {h: (sub & h) == 0 for h in (4, 2, 1)}
+
+    def combine(x, y, h):
+        m = masks[h]
+        w = jnp.where(m, y, x)
+        if h == 4:
+            moved = pltpu.roll(w, 4, 0)
+        else:
+            moved = jnp.where(m, pltpu.roll(w, 8 - h, 0), pltpu.roll(w, h, 0))
+        return jnp.where(m, x, y) + moved
+
     def pair_body(g, carry):
-        acc = jnp.zeros((8, cols), jnp.float32)
-        sub = lax.broadcasted_iota(jnp.int32, (8, cols), 0)
-        for i in range(8):
+        level = []
+        for i in (0, 4, 2, 6, 1, 5, 3, 7):
             p = g * 8 + i
-            a = pairs_s[p, 0]
-            b = pairs_s[p, 1]
-            a0 = f_ref[a, 0:LOOK_R, :]
-            a1 = f_ref[a, LOOK_R:2 * LOOK_R, :]
-            b0 = f_ref[b, 0:LOOK_R, :]
-            b1 = f_ref[b, LOOK_R:2 * LOOK_R, :]
-            cross = a1 * b0 - a0 * b1
-            row = jnp.sum(cross, axis=0, keepdims=True)
-            acc = jnp.where(sub == i, jnp.broadcast_to(row, (8, cols)), acc)
+            level.append(f_ref[pairs_s[p, 0]] * g_ref[pairs_s[p, 1]])
+        for h in (4, 2, 1):
+            level = [combine(level[2 * j], level[2 * j + 1], h) for j in range(len(level) // 2)]
         start = pl.multiple_of(g * 8, 8)
-        rows_ref[pl.ds(start, 8), :] = acc
+        rows_ref[pl.ds(start, 8), :] = level[0]
         return carry
 
     lax.fori_loop(0, n_pair // 8, pair_body, 0)
@@ -117,6 +130,7 @@
         out_specs=pl.BlockSpec(memory_space=pltpu.VMEM),
         scratch_shapes=[
             pltpu.VMEM((n_date, 2 * LOOK_R, cols), jnp.float32),
+            pltpu.VMEM((n_date, 2 * LOOK_R, cols), jnp.float32),
             pltpu.VMEM((n_pair + n_date, cols), jnp.float32),
         ],
     )(pairs, pairs, stripes, inverse)

time: 30.6 us -> 29.4 us (0.961)
  Pallas kernels: 5.34 us -> 4.14 us
    pallas_call x1, Pallas kernels: 5.34 us -> 4.14 us  [per_device(): pl.pallas_call(functools.partial(kernel, n_date, n_pair), out_shape=jax.S...]
where the time goes in v5:
time: 29.4 us; the launch traced here: 29.1 us
  waiting for transfers between devices  13.6 us (46%)
  starting transfers between devices  7.55 us (26%)
  Pallas kernels  4.14 us (14%)
  local copies, waits for them, and re-layouts  3.86 us (13%)
    all_to_all x1, waiting for transfers between devices, per_device(): got = lax.all_to_all(slc, 'date', split_axis=2, concat_axis=2, tiled=True)  13.6 us
    all_to_all x1, starting transfers between devices, per_device(): got = lax.all_to_all(slc, 'date', split_axis=2, concat_axis=2, tiled=True)  7.55 us
    pallas_call x1, Pallas kernels, per_device(): pl.pallas_call(functools.partial(kernel, n_date, n_pair), out_shape=jax.S...  4.14 us
    unnamed x6, local copies, waits for them, and re-layouts  3.86 us
  transfers between devices with their start and end apart: 1, of which 1 were waited for; matrix products, arithmetic and copies ran while one was open for 2% of the time, Pallas kernels for 0%

profile of v5, /device:TPU:0, one launch (start us, length us, event | category | flops | bytes accessed | tf_op | source)
XLA Modules:
  0.0 29.1 jit_solution(4849282295987503582)
XLA Ops:
  0.0 2.4 %copy.7 = bf16[1,2,64,2048]{3,1,0,2:T(2,128)(2,1)} copy(bf16[1,2,64,2048]{3,2,1,0:T(8,128)(2,1)} %param.3) | data formatting | bytes 1048576 | tf_op args[0]
  2.4 0.0 copy-start.1
  2.4 7.5 %all-to-all-start = ((bf16[1,2,64,2048]{3,1,0,2:T(2,128)(2,1)}), bf16[1,2,64,2048]{3,1,0,2:T(2,128)(2,1)S(1)}, u32[]{:S(2)}, u32[]{:S(2)}) async-start(bf16[1,2,64,2048]{3,1,0,2:T(2,128)(2,1)} %copy.7), calls=%async_computation | async-start | bytes 1048576 | tf_op jit(solution)/shard_map/all_to_all | solution.py:117
  9.9 0.0 copy-done.1
  9.9 0.7 %copy.8.pairs_s.pairs_v = s32[64,2]{1,0:T(8,128)} copy(s32[64,2]{0,1:T(2,128)S(1)} %copy-done.1) | data formatting | bytes 1024 | tf_op args[1]
  10.6 13.6 %all-to-all-done = bf16[1,2,64,2048]{3,1,0,2:T(2,128)(2,1)S(1)} async-done(((bf16[1,2,64,2048]{3,1,0,2:T(2,128)(2,1)}), bf16[1,2,64,2048]{3,1,0,2:T(2,128)(2,1)S(1)}, u32[]{:S(2)}, u32[]{:S(2)}) %all-to-all-start) | async-done | bytes 524320 | tf_op jit(solution)/shard_map/all_to_all | solution.py:117
  24.2 0.0 copy-start
  24.2 0.8 %copy-done = bf16[1,2,64,2048]{3,1,0,2:T(2,128)(2,1)} copy-done((bf16[1,2,64,2048]{3,1,0,2:T(2,128)(2,1)}, bf16[1,2,64,2048]{3,1,0,2:T(2,128)(2,1)S(1)}, u32[]{:S(2)}) %copy-start) | copy-done | bytes 524312
  25.0 4.1 %shard_map.37 = f32[15,1,128]{2,1,0:T(1,128)} custom-call(s32[64,2]{1,0:T(8,128)} %copy.8.pairs_s.pairs_v, s32[64,2]{1,0:T(8,128)} %copy.8.pairs_s.pairs_v, bf16[64,2,2048]{2,1,0:T(2,128)(2,1)} %bitcast.3, bf16[15,64]{1,0:T(8,128)(2,1)} %inv_ref.1), custom_call_target="tpu_custom_call" | custom-call | tf_op jit(solution)/shard_map/pallas_call | solution.py:121
Async XLA Ops:
  2.4 7.6 %copy-start.1 = (s32[64,2]{0,1:T(2,128)S(1)}, s32[64,2]{0,1:T(2,128)}, u32[]{:S(2)}) copy-start(s32[64,2]{0,1:T(2,128)} %param.4) | copy-start | bytes 1540
  2.4 21.8 %all-to-all-start = ((bf16[1,2,64,2048]{3,1,0,2:T(2,128)(2,1)}), bf16[1,2,64,2048]{3,1,0,2:T(2,128)(2,1)S(1)}, u32[]{:S(2)}, u32[]{:S(2)}) async-start(bf16[1,2,64,2048]{3,1,0,2:T(2,128)(2,1)} %copy.7), calls=%async_computation | async-start | bytes 1048576 | tf_op jit(solution)/shard_map/all_to_all | solution.py:117
  24.2 0.8 %copy-start = (bf16[1,2,64,2048]{3,1,0,2:T(2,128)(2,1)}, bf16[1,2,64,2048]{3,1,0,2:T(2,128)(2,1)S(1)}, u32[]{:S(2)}) copy-start(bf16[1,2,64,2048]{3,1,0,2:T(2,128)(2,1)S(1)} %all-to-all-done) | copy-start | bytes 1572868

commit v6 on v5

--- a/solution.py
+++ b/solution.py
@@ -39,15 +39,11 @@
         sub = lax.broadcasted_iota(jnp.int32, (8, cols), 0)
         for i in range(8):
             d = g * 8 + i
-            row = None
-            for r in range(LOOK_R):
-                v = st_ref[d * LOOK_R + r].astype(jnp.float32)
-                re = v[0:1]
-                im = v[1:2]
-                f_ref[d, r:r + 1, :] = re
-                f_ref[d, LOOK_R + r:LOOK_R + r + 1, :] = im
-                pw = re * re + im * im
-                row = pw if row is None else row + pw
+            re = st_ref[d, 0].astype(jnp.float32)
+            im = st_ref[d, 1].astype(jnp.float32)
+            f_ref[d, 0:LOOK_R, :] = re
+            f_ref[d, LOOK_R:2 * LOOK_R, :] = im
+            row = jnp.sum(re * re + im * im, axis=0, keepdims=True)
             acc = jnp.where(sub == i, jnp.broadcast_to(row, (8, cols)), acc)
         start = pl.multiple_of(n_pair + g * 8, 8)
         rows_ref[pl.ds(start, 8), :] = acc
@@ -108,14 +104,25 @@
         out_ref[s] = series[s:s + 1, :]
 
 
+def regroup_kernel(in_ref, out_ref):
+    for c in range(out_ref.shape[0]):
+        for k in range(2):
+            out_ref[c, k] = in_ref[k, c * LOOK_R:(c + 1) * LOOK_R, :]
+
+
 def per_device(slc, pairs, inverse):
     n_date = lax.axis_size("date")
     n_pair = pairs.shape[0]
     steps = inverse.shape[0]
     _, _, all_rows, cols = slc.shape
     rows = all_rows // n_date
-    got = lax.all_to_all(slc, "date", split_axis=2, concat_axis=2, tiled=True)
-    stripes = got[0].transpose(1, 0, 2)
+    chunks = pl.pallas_call(
+        regroup_kernel,
+        out_shape=jax.ShapeDtypeStruct((n_date, 2, rows, cols), slc.dtype),
+        in_specs=[pl.BlockSpec(memory_space=pltpu.VMEM)],
+        out_specs=pl.BlockSpec(memory_space=pltpu.VMEM),
+    )(slc[0])
+    stripes = lax.all_to_all(chunks, "date", split_axis=0, concat_axis=0, tiled=True)
     assert rows == LOOK_R and n_date % 8 == 0 and n_pair % 8 == 0
     looks = cols // LOOK_C
     out = pl.pallas_call(

time: 29.4 us -> 29.1 us (0.990)
  local copies, waits for them, and re-layouts: 3.86 us -> 1.49 us
  Pallas kernels: 4.14 us -> 6.19 us
    unnamed x6 -> x5, local copies, waits for them, and re-layouts: 3.86 us -> 1.49 us
    pallas_call x0 -> x1, Pallas kernels: none -> 1.97 us  [per_device(): pl.pallas_call(regroup_kernel, out_shape=jax.ShapeDtypeStruct((n_date, 2,...]
where the time goes in v6:
time: 29.1 us; the launch traced here: 28.8 us
  waiting for transfers between devices  13.6 us (47%)
  starting transfers between devices  7.55 us (26%)
  Pallas kernels  6.19 us (21%)
  local copies, waits for them, and re-layouts  1.49 us (5%)
    all_to_all x1, waiting for transfers between devices, per_device(): lax.all_to_all(chunks, 'date', split_axis=0, concat_axis=0, tiled=True)  13.6 us
    all_to_all x1, starting transfers between devices, per_device(): lax.all_to_all(chunks, 'date', split_axis=0, concat_axis=0, tiled=True)  7.55 us
    pallas_call x1, Pallas kernels, per_device(): pl.pallas_call(functools.partial(kernel, n_date, n_pair), out_shape=jax.S...  4.23 us
    pallas_call x1, Pallas kernels, per_device(): pl.pallas_call(regroup_kernel, out_shape=jax.ShapeDtypeStruct((n_date, 2,...  1.97 us
    unnamed x5, local copies, waits for them, and re-layouts  1.49 us
  transfers between devices with their start and end apart: 1, of which 1 were waited for; matrix products, arithmetic and copies ran while one was open for 2% of the time, Pallas kernels for 0%

profile of v6, /device:TPU:0, one launch (start us, length us, event | category | flops | bytes accessed | tf_op | source)
XLA Modules:
  0.0 28.8 jit_solution(2601543826607872756)
XLA Ops:
  0.0 2.0 %shard_map.37 = bf16[16,2,4,2048]{3,2,1,0:T(4,128)(2,1)} custom-call(bf16[2,64,2048]{2,1,0:T(8,128)(2,1)} %bitcast.1), custom_call_target="tpu_custom_call" | custom-call | tf_op jit(solution)/shard_map/pallas_call | solution.py:119
  2.0 0.0 copy-start.1
  2.0 7.5 %all-to-all-start = ((bf16[16,2,4,2048]{3,2,1,0:T(4,128)(2,1)}), bf16[16,2,4,2048]{3,2,1,0:T(4,128)(2,1)S(1)}, u32[]{:S(2)}, u32[]{:S(2)}) async-start(bf16[16,2,4,2048]{3,2,1,0:T(4,128)(2,1)} %shard_map.37), calls=%async_computation | async-start | bytes 1048576 | tf_op jit(solution)/shard_map/all_to_all | solution.py:125
  9.5 0.0 copy-done.1
  9.5 0.7 %copy.4.pairs_s.pairs_v = s32[64,2]{1,0:T(8,128)} copy(s32[64,2]{0,1:T(2,128)S(1)} %copy-done.1) | data formatting | bytes 1024 | tf_op args[1]
  10.2 13.6 %all-to-all-done.st_ref = bf16[16,2,4,2048]{3,2,1,0:T(4,128)(2,1)S(1)} async-done(((bf16[16,2,4,2048]{3,2,1,0:T(4,128)(2,1)}), bf16[16,2,4,2048]{3,2,1,0:T(4,128)(2,1)S(1)}, u32[]{:S(2)}, u32[]{:S(2)}) %all-to-all-start) | async-done | bytes 524320 | tf_op jit(solution)/shard_map/all_to_all | solution.py:125
  23.8 0.0 copy-start
  23.8 0.8 %copy-done = bf16[16,2,4,2048]{3,2,1,0:T(4,128)(2,1)} copy-done((bf16[16,2,4,2048]{3,2,1,0:T(4,128)(2,1)}, bf16[16,2,4,2048]{3,2,1,0:T(4,128)(2,1)S(1)}, u32[]{:S(2)}) %copy-start) | copy-done | bytes 524312
  24.6 4.2 %shard_map.38 = f32[15,1,128]{2,1,0:T(1,128)} custom-call(s32[64,2]{1,0:T(8,128)} %copy.4.pairs_s.pairs_v, s32[64,2]{1,0:T(8,128)} %copy.4.pairs_s.pairs_v, bf16[16,2,4,2048]{3,2,1,0:T(4,128)(2,1)} %copy-done, bf16[15,64]{1,0:T(8,128)(2,1)} %inv_ref.1), custom_call_target="tpu_custom_call" | custom-call | tf_op jit(solution)/shard_map/pallas_call | solution.py:128
Async XLA Ops:
  2.0 7.6 %copy-start.1 = (s32[64,2]{0,1:T(2,128)S(1)}, s32[64,2]{0,1:T(2,128)}, u32[]{:S(2)}) copy-start(s32[64,2]{0,1:T(2,128)} %param.4) | copy-start | bytes 1540
  2.0 21.8 %all-to-all-start = ((bf16[16,2,4,2048]{3,2,1,0:T(4,128)(2,1)}), bf16[16,2,4,2048]{3,2,1,0:T(4,128)(2,1)S(1)}, u32[]{:S(2)}, u32[]{:S(2)}) async-start(bf16[16,2,4,2048]{3,2,1,0:T(4,128)(2,1)} %shard_map.37), calls=%async_computation | async-start | bytes 1048576 | tf_op jit(solution)/shard_map/all_to_all | solution.py:125
  23.8 0.8 %copy-start = (bf16[16,2,4,2048]{3,2,1,0:T(4,128)(2,1)}, bf16[16,2,4,2048]{3,2,1,0:T(4,128)(2,1)S(1)}, u32[]{:S(2)}) copy-start(bf16[16,2,4,2048]{3,2,1,0:T(4,128)(2,1)S(1)} %all-to-all-done.st_ref) | copy-start | bytes 1572868

commit v7 on v6

--- a/solution.py
+++ b/solution.py
@@ -30,7 +30,8 @@
     return out
 
 
-def kernel(n_date, n_pair, pairs_s, pairs_v, st_ref, inv_ref, out_ref, f_ref, g_ref, rows_ref):
+def kernel(n_date, n_pair, pairs_s, pairs_v, st_any, inv_ref, out_ref, f_ref, g_ref, rows_ref, st_ref):
+    pltpu.sync_copy(st_any, st_ref)
     cols = st_ref.shape[-1]
     looks = cols // LOOK_C
 
@@ -131,7 +132,7 @@
         in_specs=[
             pl.BlockSpec(memory_space=pltpu.SMEM),
             pl.BlockSpec(memory_space=pltpu.VMEM),
-            pl.BlockSpec(memory_space=pltpu.VMEM),
+            pl.BlockSpec(memory_space=pl.ANY),
             pl.BlockSpec(memory_space=pltpu.VMEM),
         ],
         out_specs=pl.BlockSpec(memory_space=pltpu.VMEM),
@@ -139,7 +140,9 @@
             pltpu.VMEM((n_date, 2 * LOOK_R, cols), jnp.float32),
             pltpu.VMEM((n_date, 2 * LOOK_R, cols), jnp.float32),
             pltpu.VMEM((n_pair + n_date, cols), jnp.float32),
+            pltpu.VMEM(stripes.shape, stripes.dtype),
         ],
+        compiler_params=pltpu.CompilerParams(vmem_limit_bytes=24 * 1024 * 1024),
     )(pairs, pairs, stripes, inverse)
     return out
 

time: 29.1 us -> 28.1 us (0.966)
  local copies, waits for them, and re-layouts: 1.49 us -> 0.11 us
  waiting for transfers between devices: 13.6 us -> 14.2 us
    unnamed x5, local copies, waits for them, and re-layouts: 1.49 us -> 0.11 us
    all_to_all x1, waiting for transfers between devices: 13.6 us -> 14.2 us  [per_device(): lax.all_to_all(chunks, 'date', split_axis=0, concat_axis=0, tiled=True)]
  transfers between devices with their start and end apart: 1 -> 1, of which waited for: 1 -> 1; matrix products, arithmetic and copies ran while one was open for 2% -> 0% of each run, Pallas kernels for 0% -> 0%
where the time goes in v7:
time: 28.1 us; the launch traced here: 27.8 us
  waiting for transfers between devices  14.2 us (51%)
  starting transfers between devices  7.55 us (27%)
  Pallas kernels  5.99 us (21%)
    all_to_all x1, waiting for transfers between devices, per_device(): lax.all_to_all(chunks, 'date', split_axis=0, concat_axis=0, tiled=True)  14.2 us
    all_to_all x1, starting transfers between devices, per_device(): lax.all_to_all(chunks, 'date', split_axis=0, concat_axis=0, tiled=True)  7.55 us
    pallas_call x1, Pallas kernels, per_device(): pl.pallas_call(functools.partial(kernel, n_date, n_pair), out_shape=jax.S...  4.02 us
    pallas_call x1, Pallas kernels, per_device(): pl.pallas_call(regroup_kernel, out_shape=jax.ShapeDtypeStruct((n_date, 2,...  1.97 us
  transfers between devices with their start and end apart: 1, of which 1 were waited for; matrix products, arithmetic and copies ran while one was open for 0% of the time, Pallas kernels for 0%

profile of v7, /device:TPU:0, one launch (start us, length us, event | category | flops | bytes accessed | tf_op | source)
XLA Modules:
  0.0 27.8 jit_solution(11868815832377654162)
XLA Ops:
  0.0 2.0 %shard_map.37 = bf16[16,2,4,2048]{3,2,1,0:T(4,128)(2,1)} custom-call(bf16[2,64,2048]{2,1,0:T(8,128)(2,1)} %bitcast.1), custom_call_target="tpu_custom_call" | custom-call | tf_op jit(solution)/shard_map/pallas_call | solution.py:120
  2.0 0.0 copy-start.1
  2.0 7.5 %all-to-all-start = ((bf16[16,2,4,2048]{3,2,1,0:T(4,128)(2,1)}), bf16[16,2,4,2048]{3,2,1,0:T(4,128)(2,1)S(1)}, u32[]{:S(2)}, u32[]{:S(2)}) async-start(bf16[16,2,4,2048]{3,2,1,0:T(4,128)(2,1)} %shard_map.37), calls=%async_computation | async-start | bytes 1048576 | tf_op jit(solution)/shard_map/all_to_all | solution.py:126
  9.5 0.0 copy-done.1
  9.5 0.0 copy-start
  9.5 0.1 copy.4.pairs_s.pairs_v
  9.6 14.2 %all-to-all-done.st_any = bf16[16,2,4,2048]{3,2,1,0:T(4,128)(2,1)S(1)} async-done(((bf16[16,2,4,2048]{3,2,1,0:T(4,128)(2,1)}), bf16[16,2,4,2048]{3,2,1,0:T(4,128)(2,1)S(1)}, u32[]{:S(2)}, u32[]{:S(2)}) %all-to-all-start) | async-done | bytes 524320 | tf_op jit(solution)/shard_map/all_to_all | solution.py:126
  23.8 0.0 copy-done
  23.8 4.0 %shard_map.38 = f32[15,1,128]{2,1,0:T(1,128)} custom-call(s32[64,2]{1,0:T(8,128)S(1)} %copy.4.pairs_s.pairs_v, s32[64,2]{1,0:T(8,128)S(1)} %copy.4.pairs_s.pairs_v, bf16[16,2,4,2048]{3,2,1,0:T(4,128)(2,1)S(1)} %all-to-all-done.st_any, bf16[15,64]{1,0:T(8,128)(2,1)S(1)} %copy-done), custom_call_target="tpu_custom_call" | custom-call | tf_op jit(solution)/shard_map/pallas_call | solution.py:129
Async XLA Ops:
  2.0 7.6 %copy-start.1 = (s32[64,2]{0,1:T(2,128)S(1)}, s32[64,2]{0,1:T(2,128)}, u32[]{:S(2)}) copy-start(s32[64,2]{0,1:T(2,128)} %param.4) | copy-start | bytes 1540
  2.0 21.8 %all-to-all-start = ((bf16[16,2,4,2048]{3,2,1,0:T(4,128)(2,1)}), bf16[16,2,4,2048]{3,2,1,0:T(4,128)(2,1)S(1)}, u32[]{:S(2)}, u32[]{:S(2)}) async-start(bf16[16,2,4,2048]{3,2,1,0:T(4,128)(2,1)} %shard_map.37), calls=%async_computation | async-start | bytes 1048576 | tf_op jit(solution)/shard_map/all_to_all | solution.py:126
  9.5 14.3 %copy-start = (bf16[15,64]{1,0:T(8,128)(2,1)S(1)}, bf16[15,64]{1,0:T(8,128)(2,1)}, u32[]{:S(2)}) copy-start(bf16[15,64]{1,0:T(8,128)(2,1)} %inv_ref.1) | copy-start | bytes 5764

commit v8 on v6

--- a/solution.py
+++ b/solution.py
@@ -121,6 +121,7 @@
         out_shape=jax.ShapeDtypeStruct((n_date, 2, rows, cols), slc.dtype),
         in_specs=[pl.BlockSpec(memory_space=pltpu.VMEM)],
         out_specs=pl.BlockSpec(memory_space=pltpu.VMEM),
+        compiler_params=pltpu.CompilerParams(vmem_limit_bytes=8 * 1024 * 1024),
     )(slc[0])
     stripes = lax.all_to_all(chunks, "date", split_axis=0, concat_axis=0, tiled=True)
     assert rows == LOOK_R and n_date % 8 == 0 and n_pair % 8 == 0
@@ -140,6 +141,7 @@
             pltpu.VMEM((n_date, 2 * LOOK_R, cols), jnp.float32),
             pltpu.VMEM((n_pair + n_date, cols), jnp.float32),
         ],
+        compiler_params=pltpu.CompilerParams(vmem_limit_bytes=24 * 1024 * 1024),
     )(pairs, pairs, stripes, inverse)
     return out
 

time: 29.1 us -> 28 us (0.962)
  Pallas kernels: 6.19 us -> 4.9 us
  waiting for transfers between devices: 13.6 us -> 14.2 us
  local copies, waits for them, and re-layouts: 1.49 us -> 1.15 us
    pallas_call x1, Pallas kernels: 1.97 us -> 0.93 us  [per_device(): pl.pallas_call(regroup_kernel, out_shape=jax.ShapeDtypeStruct((n_date, 2,...]
    all_to_all x1, waiting for transfers between devices: 13.6 us -> 14.2 us  [per_device(): lax.all_to_all(chunks, 'date', split_axis=0, concat_axis=0, tiled=True)]
    unnamed x5 -> x7, local copies, waits for them, and re-layouts: 1.49 us -> 1.15 us
  transfers between devices with their start and end apart: 1 -> 1, of which waited for: 1 -> 1; matrix products, arithmetic and copies ran while one was open for 2% -> 0% of each run, Pallas kernels for 0% -> 0%
where the time goes in v8:
time: 28 us; the launch traced here: 27.8 us
  waiting for transfers between devices  14.2 us (51%)
  starting transfers between devices  7.55 us (27%)
  Pallas kernels  4.9 us (18%)
  local copies, waits for them, and re-layouts  1.15 us (4%)
    all_to_all x1, waiting for transfers between devices, per_device(): lax.all_to_all(chunks, 'date', split_axis=0, concat_axis=0, tiled=True)  14.2 us
    all_to_all x1, starting transfers between devices, per_device(): lax.all_to_all(chunks, 'date', split_axis=0, concat_axis=0, tiled=True)  7.55 us
    pallas_call x1, Pallas kernels, per_device(): pl.pallas_call(functools.partial(kernel, n_date, n_pair), out_shape=jax.S...  3.97 us
    unnamed x7, local copies, waits for them, and re-layouts  1.15 us
    pallas_call x1, Pallas kernels, per_device(): pl.pallas_call(regroup_kernel, out_shape=jax.ShapeDtypeStruct((n_date, 2,...  0.93 us
  transfers between devices with their start and end apart: 1, of which 1 were waited for; matrix products, arithmetic and copies ran while one was open for 0% of the time, Pallas kernels for 0%

profile of v8, /device:TPU:0, one launch (start us, length us, event | category | flops | bytes accessed | tf_op | source)
XLA Modules:
  0.0 27.8 jit_solution(5999664840575360525)
XLA Ops:
  0.0 0.0 copy-start
  0.0 1.0 %copy-done = bf16[1,2,64,2048]{3,2,1,0:T(8,128)(2,1)S(1)} copy-done((bf16[1,2,64,2048]{3,2,1,0:T(8,128)(2,1)S(1)}, bf16[1,2,64,2048]{3,2,1,0:T(8,128)(2,1)}, u32[]{:S(2)}) %copy-start) | copy-done | bytes 524312
  1.0 0.9 %shard_map.37 = bf16[16,2,4,2048]{3,2,1,0:T(4,128)(2,1)} custom-call(bf16[2,64,2048]{2,1,0:T(8,128)(2,1)S(1)} %bitcast.1), custom_call_target="tpu_custom_call" | custom-call | tf_op jit(solution)/shard_map/pallas_call | solution.py:119
  2.0 0.0 copy-start.2
  2.0 7.5 %all-to-all-start = ((bf16[16,2,4,2048]{3,2,1,0:T(4,128)(2,1)}), bf16[16,2,4,2048]{3,2,1,0:T(4,128)(2,1)S(1)}, u32[]{:S(2)}, u32[]{:S(2)}) async-start(bf16[16,2,4,2048]{3,2,1,0:T(4,128)(2,1)} %shard_map.37), calls=%async_computation | async-start | bytes 1048576 | tf_op jit(solution)/shard_map/all_to_all | solution.py:126
  9.5 0.0 copy-done.2
  9.5 0.0 copy-start.1
  9.6 0.1 copy.4.pairs_s.pairs_v
  9.7 14.2 %all-to-all-done.st_ref = bf16[16,2,4,2048]{3,2,1,0:T(4,128)(2,1)S(1)} async-done(((bf16[16,2,4,2048]{3,2,1,0:T(4,128)(2,1)}), bf16[16,2,4,2048]{3,2,1,0:T(4,128)(2,1)S(1)}, u32[]{:S(2)}, u32[]{:S(2)}) %all-to-all-start) | async-done | bytes 524320 | tf_op jit(solution)/shard_map/all_to_all | solution.py:126
  23.8 0.0 copy-done.1
  23.8 4.0 %shard_map.38 = f32[15,1,128]{2,1,0:T(1,128)} custom-call(s32[64,2]{1,0:T(8,128)S(1)} %copy.4.pairs_s.pairs_v, s32[64,2]{1,0:T(8,128)S(1)} %copy.4.pairs_s.pairs_v, bf16[16,2,4,2048]{3,2,1,0:T(4,128)(2,1)S(1)} %all-to-all-done.st_ref, bf16[15,64]{1,0:T(8,128)(2,1)S(1)} %copy-done.1), custom_call_target="tpu_custom_call" | custom-call | tf_op jit(solution)/shard_map/pallas_call | solution.py:129
Async XLA Ops:
  0.0 1.0 %copy-start = (bf16[1,2,64,2048]{3,2,1,0:T(8,128)(2,1)S(1)}, bf16[1,2,64,2048]{3,2,1,0:T(8,128)(2,1)}, u32[]{:S(2)}) copy-start(bf16[1,2,64,2048]{3,2,1,0:T(8,128)(2,1)} %param.3) | copy-start | bytes 1572868
  2.0 7.6 %copy-start.2 = (s32[64,2]{0,1:T(2,128)S(1)}, s32[64,2]{0,1:T(2,128)}, u32[]{:S(2)}) copy-start(s32[64,2]{0,1:T(2,128)} %param.4) | copy-start | bytes 1540
  2.0 21.8 %all-to-all-start = ((bf16[16,2,4,2048]{3,2,1,0:T(4,128)(2,1)}), bf16[16,2,4,2048]{3,2,1,0:T(4,128)(2,1)S(1)}, u32[]{:S(2)}, u32[]{:S(2)}) async-start(bf16[16,2,4,2048]{3,2,1,0:T(4,128)(2,1)} %shard_map.37), calls=%async_computation | async-start | bytes 1048576 | tf_op jit(solution)/shard_map/all_to_all | solution.py:126
  9.5 14.3 %copy-start.1 = (bf16[15,64]{1,0:T(8,128)(2,1)S(1)}, bf16[15,64]{1,0:T(8,128)(2,1)}, u32[]{:S(2)}) copy-start(bf16[15,64]{1,0:T(8,128)(2,1)} %inv_ref.1) | copy-start | bytes 5764

commit v9 on v8

--- a/solution.py
+++ b/solution.py
@@ -30,26 +30,16 @@
     return out
 
 
-def kernel(n_date, n_pair, pairs_s, pairs_v, st_ref, inv_ref, out_ref, f_ref, g_ref, rows_ref):
+def kernel(n_date, n_pair, pairs_s, pairs_v, st_ref, inv_ref, window_ref, out_ref, f_ref, g_ref, rows_ref):
     cols = st_ref.shape[-1]
     looks = cols // LOOK_C
 
-    def date_body(g, carry):
-        acc = jnp.zeros((8, cols), jnp.float32)
-        sub = lax.broadcasted_iota(jnp.int32, (8, cols), 0)
-        for i in range(8):
-            d = g * 8 + i
-            re = st_ref[d, 0].astype(jnp.float32)
-            im = st_ref[d, 1].astype(jnp.float32)
-            f_ref[d, 0:LOOK_R, :] = re
-            f_ref[d, LOOK_R:2 * LOOK_R, :] = im
-            row = jnp.sum(re * re + im * im, axis=0, keepdims=True)
-            acc = jnp.where(sub == i, jnp.broadcast_to(row, (8, cols)), acc)
-        start = pl.multiple_of(n_pair + g * 8, 8)
-        rows_ref[pl.ds(start, 8), :] = acc
+    def date_body(d, carry):
+        f_ref[d, 0:LOOK_R, :] = st_ref[d, 0].astype(jnp.float32)
+        f_ref[d, LOOK_R:2 * LOOK_R, :] = st_ref[d, 1].astype(jnp.float32)
         return carry
 
-    lax.fori_loop(0, n_date // 8, date_body, 0)
+    lax.fori_loop(0, n_date, date_body, 0)
 
     sub = lax.broadcasted_iota(jnp.int32, (2 * LOOK_R, cols), 0)
     sign = jnp.where(sub < LOOK_R, -1.0, 1.0).astype(jnp.float32)
@@ -71,6 +61,19 @@
             moved = jnp.where(m, pltpu.roll(w, 8 - h, 0), pltpu.roll(w, h, 0))
         return jnp.where(m, x, y) + moved
 
+    def power_body(g, carry):
+        level = []
+        for i in (0, 4, 2, 6, 1, 5, 3, 7):
+            x = f_ref[g * 8 + i]
+            level.append(x * x)
+        for h in (4, 2, 1):
+            level = [combine(level[2 * j], level[2 * j + 1], h) for j in range(len(level) // 2)]
+        start = pl.multiple_of(n_pair + g * 8, 8)
+        rows_ref[pl.ds(start, 8), :] = level[0]
+        return carry
+
+    lax.fori_loop(0, n_date // 8, power_body, 0)
+
     def pair_body(g, carry):
         level = []
         for i in (0, 4, 2, 6, 1, 5, 3, 7):
@@ -84,10 +87,7 @@
 
     lax.fori_loop(0, n_pair // 8, pair_body, 0)
 
-    c_idx = lax.broadcasted_iota(jnp.int32, (cols, looks), 0)
-    j_idx = lax.broadcasted_iota(jnp.int32, (cols, looks), 1)
-    window = ((c_idx >= j_idx * LOOK_C) & (c_idx < j_idx * LOOK_C + LOOK_C)).astype(jnp.bfloat16)
-    looked = dot3(split3(rows_ref[...]), window, True)
+    looked = dot3(split3(rows_ref[...]), window_ref[...], True)
     looked_cross = looked[0:n_pair]
     looked_pow = looked[n_pair:n_pair + n_date]
 
@@ -126,11 +126,14 @@
     stripes = lax.all_to_all(chunks, "date", split_axis=0, concat_axis=0, tiled=True)
     assert rows == LOOK_R and n_date % 8 == 0 and n_pair % 8 == 0
     looks = cols // LOOK_C
+    col = lax.broadcasted_iota(jnp.int32, (cols, looks), 0) // LOOK_C
+    window = (col == lax.broadcasted_iota(jnp.int32, (cols, looks), 1)).astype(jnp.bfloat16)
     out = pl.pallas_call(
         functools.partial(kernel, n_date, n_pair),
         out_shape=jax.ShapeDtypeStruct((steps, 1, looks), jnp.float32),
         in_specs=[
             pl.BlockSpec(memory_space=pltpu.SMEM),
+            pl.BlockSpec(memory_space=pltpu.VMEM),
             pl.BlockSpec(memory_space=pltpu.VMEM),
             pl.BlockSpec(memory_space=pltpu.VMEM),
             pl.BlockSpec(memory_space=pltpu.VMEM),
@@ -142,7 +145,7 @@
             pltpu.VMEM((n_pair + n_date, cols), jnp.float32),
         ],
         compiler_params=pltpu.CompilerParams(vmem_limit_bytes=24 * 1024 * 1024),
-    )(pairs, pairs, stripes, inverse)
+    )(pairs, pairs, stripes, inverse, window)
     return out
 
 

time: 28 us -> 27.8 us (level)
  waiting for transfers between devices: 14.2 us -> 12.4 us
  other arithmetic: 0 us -> 1.71 us
    all_to_all x1, waiting for transfers between devices: 14.2 us -> 12.4 us  [per_device(): lax.all_to_all(chunks, 'date', split_axis=0, concat_axis=0, tiled=True)]
    convert_element_type x0 -> x1, other arithmetic: none -> 1.7 us  [per_device(): (col == lax.broadcasted_iota(jnp.int32, (cols, looks), 1)).astype(jnp.bfl...]
  transfers between devices with their start and end apart: 1 -> 1, of which waited for: 1 -> 1; matrix products, arithmetic and copies ran while one was open for 0% -> 7% of each run, Pallas kernels for 0% -> 0%
where the time goes in v9:
time: 27.8 us; the launch traced here: 27.5 us
  waiting for transfers between devices  12.4 us (45%)
  starting transfers between devices  7.55 us (27%)
  Pallas kernels  4.67 us (17%)
  other arithmetic  1.71 us (6%)
  local copies, waits for them, and re-layouts  1.15 us (4%)
    all_to_all x1, waiting for transfers between devices, per_device(): lax.all_to_all(chunks, 'date', split_axis=0, concat_axis=0, tiled=True)  12.4 us
    all_to_all x1, starting transfers between devices, per_device(): lax.all_to_all(chunks, 'date', split_axis=0, concat_axis=0, tiled=True)  7.55 us
    pallas_call x1, Pallas kernels, per_device(): pl.pallas_call(functools.partial(kernel, n_date, n_pair), out_shape=jax.S...  3.75 us
    convert_element_type x1, other arithmetic, per_device(): (col == lax.broadcasted_iota(jnp.int32, (cols, looks), 1)).astype(jnp.bfl...  1.7 us
    unnamed x7, local copies, waits for them, and re-layouts  1.15 us
    pallas_call x1, Pallas kernels, per_device(): pl.pallas_call(regroup_kernel, out_shape=jax.ShapeDtypeStruct((n_date, 2,...  0.92 us
  transfers between devices with their start and end apart: 1, of which 1 were waited for; matrix products, arithmetic and copies ran while one was open for 7% of the time, Pallas kernels for 0%

profile of v9, /device:TPU:0, one launch (start us, length us, event | category | flops | bytes accessed | tf_op | source)
XLA Modules:
  0.0 27.5 jit_solution(16072432602066427018)
XLA Ops:
  0.0 0.0 copy-start
  0.0 1.0 %copy-done = bf16[1,2,64,2048]{3,2,1,0:T(8,128)(2,1)S(1)} copy-done((bf16[1,2,64,2048]{3,2,1,0:T(8,128)(2,1)S(1)}, bf16[1,2,64,2048]{3,2,1,0:T(8,128)(2,1)}, u32[]{:S(2)}) %copy-start) | copy-done | bytes 524312
  1.0 0.9 %shard_map.37 = bf16[16,2,4,2048]{3,2,1,0:T(4,128)(2,1)} custom-call(bf16[2,64,2048]{2,1,0:T(8,128)(2,1)S(1)} %bitcast.1), custom_call_target="tpu_custom_call" | custom-call | tf_op jit(solution)/shard_map/pallas_call | solution.py:119
  2.0 0.0 copy-start.2
  2.0 7.5 %all-to-all-start = ((bf16[16,2,4,2048]{3,2,1,0:T(4,128)(2,1)}), bf16[16,2,4,2048]{3,2,1,0:T(4,128)(2,1)S(1)}, u32[]{:S(2)}, u32[]{:S(2)}) async-start(bf16[16,2,4,2048]{3,2,1,0:T(4,128)(2,1)} %shard_map.37), calls=%async_computation | async-start | bytes 1048576 | tf_op jit(solution)/shard_map/all_to_all | solution.py:126
  9.5 0.0 copy-done.2
  9.5 0.1 copy.4.pairs_s.pairs_v
  9.6 0.0 copy-start.1
  9.7 1.7 %fusion.window_ref = bf16[2048,128]{1,0:T(8,128)(2,1)S(1)} fusion(s32[2048]{0:T(1024)S(1)} %get-tuple-element.5, s32[2048]{0:T(1024)S(1)} %get-tuple-element.6, pred[2048]{0:T(1024)(128)(4,1)S(1)} %fusion.3), kind=kLoop, calls=%fused_computation.1 | loop fusion | flops 786432 | bytes 542720 | tf_op jit(solution)/shard_map/convert_element_type | solution.py:130
  11.4 12.4 %all-to-all-done.st_ref = bf16[16,2,4,2048]{3,2,1,0:T(4,128)(2,1)S(1)} async-done(((bf16[16,2,4,2048]{3,2,1,0:T(4,128)(2,1)}), bf16[16,2,4,2048]{3,2,1,0:T(4,128)(2,1)S(1)}, u32[]{:S(2)}, u32[]{:S(2)}) %all-to-all-start) | async-done | bytes 524320 | tf_op jit(solution)/shard_map/all_to_all | solution.py:126
  23.8 0.0 copy-done.1
  23.8 3.7 %shard_map.38 = f32[15,1,128]{2,1,0:T(1,128)} custom-call(s32[64,2]{1,0:T(8,128)S(1)} %copy.4.pairs_s.pairs_v, s32[64,2]{1,0:T(8,128)S(1)} %copy.4.pairs_s.pairs_v, bf16[16,2,4,2048]{3,2,1,0:T(4,128)(2,1)S(1)} %all-to-all-done.st_ref, bf16[15,64]{1,0:T(8,128)(2,1)S(1)} %copy-done.1, bf16[2048,128]{1,0:T(8,128)(2,1)S(1)} %fusion.window_ref), custom_call_target="tpu_custom_call" | custom-call | tf_op jit(solution)/shard_map/pallas_call | solution.py:131
  (2 shorter events, 0.0 us)
Async XLA Ops:
  0.0 1.0 %copy-start = (bf16[1,2,64,2048]{3,2,1,0:T(8,128)(2,1)S(1)}, bf16[1,2,64,2048]{3,2,1,0:T(8,128)(2,1)}, u32[]{:S(2)}) copy-start(bf16[1,2,64,2048]{3,2,1,0:T(8,128)(2,1)} %param.3) | copy-start | bytes 1572868
  2.0 7.6 %copy-start.2 = (s32[64,2]{0,1:T(2,128)S(1)}, s32[64,2]{0,1:T(2,128)}, u32[]{:S(2)}) copy-start(s32[64,2]{0,1:T(2,128)} %param.4) | copy-start | bytes 1540
  2.0 21.8 %all-to-all-start = ((bf16[16,2,4,2048]{3,2,1,0:T(4,128)(2,1)}), bf16[16,2,4,2048]{3,2,1,0:T(4,128)(2,1)S(1)}, u32[]{:S(2)}, u32[]{:S(2)}) async-start(bf16[16,2,4,2048]{3,2,1,0:T(4,128)(2,1)} %shard_map.37), calls=%async_computation | async-start | bytes 1048576 | tf_op jit(solution)/shard_map/all_to_all | solution.py:126
  9.6 14.1 %copy-start.1 = (bf16[15,64]{1,0:T(8,128)(2,1)S(1)}, bf16[15,64]{1,0:T(8,128)(2,1)}, u32[]{:S(2)}) copy-start(bf16[15,64]{1,0:T(8,128)(2,1)} %inv_ref.1) | copy-start | bytes 5764

commit v10 on v9

--- a/solution.py
+++ b/solution.py
@@ -35,8 +35,7 @@
     looks = cols // LOOK_C
 
     def date_body(d, carry):
-        f_ref[d, 0:LOOK_R, :] = st_ref[d, 0].astype(jnp.float32)
-        f_ref[d, LOOK_R:2 * LOOK_R, :] = st_ref[d, 1].astype(jnp.float32)
+        f_ref[d] = st_ref[d].astype(jnp.float32)
         return carry
 
     lax.fori_loop(0, n_date, date_body, 0)
@@ -107,7 +106,7 @@
 def regroup_kernel(in_ref, out_ref):
     for c in range(out_ref.shape[0]):
         for k in range(2):
-            out_ref[c, k] = in_ref[k, c * LOOK_R:(c + 1) * LOOK_R, :]
+            out_ref[c, k * LOOK_R:(k + 1) * LOOK_R, :] = in_ref[k, c * LOOK_R:(c + 1) * LOOK_R, :]
 
 
 def per_device(slc, pairs, inverse):
@@ -118,7 +117,7 @@
     rows = all_rows // n_date
     chunks = pl.pallas_call(
         regroup_kernel,
-        out_shape=jax.ShapeDtypeStruct((n_date, 2, rows, cols), slc.dtype),
+        out_shape=jax.ShapeDtypeStruct((n_date, 2 * rows, cols), slc.dtype),
         in_specs=[pl.BlockSpec(memory_space=pltpu.VMEM)],
         out_specs=pl.BlockSpec(memory_space=pltpu.VMEM),
         compiler_params=pltpu.CompilerParams(vmem_limit_bytes=8 * 1024 * 1024),

time: 27.8 us -> 27.7 us (level)
  no operation moved by 1% of the time
where the time goes in v10:
time: 27.7 us; the launch traced here: 27.4 us
  waiting for transfers between devices  12.4 us (45%)
  starting transfers between devices  7.55 us (27%)
  Pallas kernels  4.57 us (16%)
  other arithmetic  1.71 us (6%)
  local copies, waits for them, and re-layouts  1.15 us (4%)
    all_to_all x1, waiting for transfers between devices, per_device(): lax.all_to_all(chunks, 'date', split_axis=0, concat_axis=0, tiled=True)  12.4 us
    all_to_all x1, starting transfers between devices, per_device(): lax.all_to_all(chunks, 'date', split_axis=0, concat_axis=0, tiled=True)  7.55 us
    pallas_call x1, Pallas kernels, per_device(): pl.pallas_call(functools.partial(kernel, n_date, n_pair), out_shape=jax.S...  3.68 us
    convert_element_type x1, other arithmetic, per_device(): (col == lax.broadcasted_iota(jnp.int32, (cols, looks), 1)).astype(jnp.bfl...  1.7 us
    unnamed x7, local copies, waits for them, and re-layouts  1.15 us
    pallas_call x1, Pallas kernels, per_device(): pl.pallas_call(regroup_kernel, out_shape=jax.ShapeDtypeStruct((n_date, 2...  0.89 us
  transfers between devices with their start and end apart: 1, of which 1 were waited for; matrix products, arithmetic and copies ran while one was open for 7% of the time, Pallas kernels for 0%

profile of v10, /device:TPU:0, one launch (start us, length us, event | category | flops | bytes accessed | tf_op | source)
XLA Modules:
  0.0 27.4 jit_solution(7175839689507793884)
XLA Ops:
  0.0 0.0 copy-start
  0.0 1.0 %copy-done = bf16[1,2,64,2048]{3,2,1,0:T(8,128)(2,1)S(1)} copy-done((bf16[1,2,64,2048]{3,2,1,0:T(8,128)(2,1)S(1)}, bf16[1,2,64,2048]{3,2,1,0:T(8,128)(2,1)}, u32[]{:S(2)}) %copy-start) | copy-done | bytes 524312
  1.0 0.9 %shard_map.37 = bf16[16,8,2048]{2,1,0:T(8,128)(2,1)} custom-call(bf16[2,64,2048]{2,1,0:T(8,128)(2,1)S(1)} %bitcast.1), custom_call_target="tpu_custom_call" | custom-call | tf_op jit(solution)/shard_map/pallas_call | solution.py:118
  1.9 0.0 copy-start.2
  1.9 7.5 %all-to-all-start = ((bf16[16,8,2048]{2,1,0:T(8,128)(2,1)}), bf16[16,8,2048]{2,1,0:T(8,128)(2,1)S(1)}, u32[]{:S(2)}, u32[]{:S(2)}) async-start(bf16[16,8,2048]{2,1,0:T(8,128)(2,1)} %shard_map.37), calls=%async_computation | async-start | bytes 1048576 | tf_op jit(solution)/shard_map/all_to_all | solution.py:125
  9.5 0.0 copy-done.2
  9.5 0.1 copy.4.pairs_s.pairs_v
  9.6 0.0 copy-start.1
  9.6 1.7 %fusion.window_ref = bf16[2048,128]{1,0:T(8,128)(2,1)S(1)} fusion(s32[2048]{0:T(1024)S(1)} %get-tuple-element.5, s32[2048]{0:T(1024)S(1)} %get-tuple-element.6, pred[2048]{0:T(1024)(128)(4,1)S(1)} %fusion.3), kind=kLoop, calls=%fused_computation.1 | loop fusion | flops 786432 | bytes 542720 | tf_op jit(solution)/shard_map/convert_element_type | solution.py:129
  11.3 12.4 %all-to-all-done.st_ref = bf16[16,8,2048]{2,1,0:T(8,128)(2,1)S(1)} async-done(((bf16[16,8,2048]{2,1,0:T(8,128)(2,1)}), bf16[16,8,2048]{2,1,0:T(8,128)(2,1)S(1)}, u32[]{:S(2)}, u32[]{:S(2)}) %all-to-all-start) | async-done | bytes 524320 | tf_op jit(solution)/shard_map/all_to_all | solution.py:125
  23.8 0.0 copy-done.1
  23.8 3.7 %shard_map.38 = f32[15,1,128]{2,1,0:T(1,128)} custom-call(s32[64,2]{1,0:T(8,128)S(1)} %copy.4.pairs_s.pairs_v, s32[64,2]{1,0:T(8,128)S(1)} %copy.4.pairs_s.pairs_v, bf16[16,8,2048]{2,1,0:T(8,128)(2,1)S(1)} %all-to-all-done.st_ref, bf16[15,64]{1,0:T(8,128)(2,1)S(1)} %copy-done.1, bf16[2048,128]{1,0:T(8,128)(2,1)S(1)} %fusion.window_ref), custom_call_target="tpu_custom_call" | custom-call | tf_op jit(solution)/shard_map/pallas_call | solution.py:130
  (2 shorter events, 0.0 us)
Async XLA Ops:
  0.0 1.0 %copy-start = (bf16[1,2,64,2048]{3,2,1,0:T(8,128)(2,1)S(1)}, bf16[1,2,64,2048]{3,2,1,0:T(8,128)(2,1)}, u32[]{:S(2)}) copy-start(bf16[1,2,64,2048]{3,2,1,0:T(8,128)(2,1)} %param.3) | copy-start | bytes 1572868
  1.9 7.6 %copy-start.2 = (s32[64,2]{0,1:T(2,128)S(1)}, s32[64,2]{0,1:T(2,128)}, u32[]{:S(2)}) copy-start(s32[64,2]{0,1:T(2,128)} %param.4) | copy-start | bytes 1540
  1.9 21.8 %all-to-all-start = ((bf16[16,8,2048]{2,1,0:T(8,128)(2,1)}), bf16[16,8,2048]{2,1,0:T(8,128)(2,1)S(1)}, u32[]{:S(2)}, u32[]{:S(2)}) async-start(bf16[16,8,2048]{2,1,0:T(8,128)(2,1)} %shard_map.37), calls=%async_computation | async-start | bytes 1048576 | tf_op jit(solution)/shard_map/all_to_all | solution.py:125
  9.6 14.1 %copy-start.1 = (bf16[15,64]{1,0:T(8,128)(2,1)S(1)}, bf16[15,64]{1,0:T(8,128)(2,1)}, u32[]{:S(2)}) copy-start(bf16[15,64]{1,0:T(8,128)(2,1)} %inv_ref.1) | copy-start | bytes 5764

commit v11 on v10

--- a/solution.py
+++ b/solution.py
@@ -103,10 +103,22 @@
         out_ref[s] = series[s:s + 1, :]
 
 
-def regroup_kernel(in_ref, out_ref):
-    for c in range(out_ref.shape[0]):
-        for k in range(2):
-            out_ref[c, k * LOOK_R:(k + 1) * LOOK_R, :] = in_ref[k, c * LOOK_R:(c + 1) * LOOK_R, :]
+def regroup_kernel(in_hbm, out_ref, in_ref, sems):
+    n_chunk = out_ref.shape[0]
+    half = n_chunk // 2
+    rows_half = half * LOOK_R
+    copies = []
+    for k in range(2):
+        for q in range(2):
+            rows = pl.ds(q * rows_half, rows_half)
+            copy = pltpu.make_async_copy(in_hbm.at[k, rows], in_ref.at[k, rows], sems.at[2 * k + q])
+            copy.start()
+            copies.append(copy)
+    for k in range(2):
+        for q in range(2):
+            copies[2 * k + q].wait()
+            for c in range(q * half, (q + 1) * half):
+                out_ref[c, k * LOOK_R:(k + 1) * LOOK_R, :] = in_ref[k, c * LOOK_R:(c + 1) * LOOK_R, :]
 
 
 def per_device(slc, pairs, inverse):
@@ -118,9 +130,9 @@
     chunks = pl.pallas_call(
         regroup_kernel,
         out_shape=jax.ShapeDtypeStruct((n_date, 2 * rows, cols), slc.dtype),
-        in_specs=[pl.BlockSpec(memory_space=pltpu.VMEM)],
+        in_specs=[pl.BlockSpec(memory_space=pl.ANY)],
         out_specs=pl.BlockSpec(memory_space=pltpu.VMEM),
-        compiler_params=pltpu.CompilerParams(vmem_limit_bytes=8 * 1024 * 1024),
+        scratch_shapes=[pltpu.VMEM(slc.shape[1:], slc.dtype), pltpu.SemaphoreType.DMA((4,))],
     )(slc[0])
     stripes = lax.all_to_all(chunks, "date", split_axis=0, concat_axis=0, tiled=True)
     assert rows == LOOK_R and n_date % 8 == 0 and n_pair % 8 == 0

time: 27.7 us -> 27.6 us (level)
  Pallas kernels: 4.57 us -> 5.63 us
  local copies, waits for them, and re-layouts: 1.15 us -> 0.11 us
    pallas_call x1, Pallas kernels: 0.89 us -> 1.95 us  [per_device(): pl.pallas_call(regroup_kernel, out_shape=jax.ShapeDtypeStruct((n_date, 2...]
    unnamed x7 -> x5, local copies, waits for them, and re-layouts: 1.15 us -> 0.11 us
where the time goes in v11:
time: 27.6 us; the launch traced here: 27.4 us
  waiting for transfers between devices  12.4 us (45%)
  starting transfers between devices  7.43 us (27%)
  Pallas kernels  5.63 us (20%)
  other arithmetic  1.71 us (6%)
    all_to_all x1, waiting for transfers between devices, per_device(): lax.all_to_all(chunks, 'date', split_axis=0, concat_axis=0, tiled=True)  12.4 us
    all_to_all x1, starting transfers between devices, per_device(): lax.all_to_all(chunks, 'date', split_axis=0, concat_axis=0, tiled=True)  7.43 us
    pallas_call x1, Pallas kernels, per_device(): pl.pallas_call(functools.partial(kernel, n_date, n_pair), out_shape=jax.S...  3.68 us
    pallas_call x1, Pallas kernels, per_device(): pl.pallas_call(regroup_kernel, out_shape=jax.ShapeDtypeStruct((n_date, 2...  1.95 us
    convert_element_type x1, other arithmetic, per_device(): (col == lax.broadcasted_iota(jnp.int32, (cols, looks), 1)).astype(jnp.bfl...  1.7 us
  transfers between devices with their start and end apart: 1, of which 1 were waited for; matrix products, arithmetic and copies ran while one was open for 7% of the time, Pallas kernels for 0%

profile of v11, /device:TPU:0, one launch (start us, length us, event | category | flops | bytes accessed | tf_op | source)
XLA Modules:
  0.0 27.4 jit_solution(15539811436585933460)
XLA Ops:
  0.0 1.9 %shard_map.37 = bf16[16,8,2048]{2,1,0:T(8,128)(2,1)} custom-call(bf16[2,64,2048]{2,1,0:T(8,128)(2,1)} %bitcast.1), custom_call_target="tpu_custom_call" | custom-call | tf_op jit(solution)/shard_map/pallas_call | solution.py:130
  2.0 0.0 copy-start.1
  2.0 7.4 %all-to-all-start = ((bf16[16,8,2048]{2,1,0:T(8,128)(2,1)}), bf16[16,8,2048]{2,1,0:T(8,128)(2,1)S(1)}, u32[]{:S(2)}, u32[]{:S(2)}) async-start(bf16[16,8,2048]{2,1,0:T(8,128)(2,1)} %shard_map.37), calls=%async_computation | async-start | bytes 1048576 | tf_op jit(solution)/shard_map/all_to_all | solution.py:137
  9.4 0.0 copy-done.1
  9.4 0.1 copy.4.pairs_s.pairs_v
  9.5 0.0 copy-start
  9.5 1.7 %fusion.window_ref = bf16[2048,128]{1,0:T(8,128)(2,1)S(1)} fusion(s32[2048]{0:T(1024)S(1)} %get-tuple-element.5, s32[2048]{0:T(1024)S(1)} %get-tuple-element.6, pred[2048]{0:T(1024)(128)(4,1)S(1)} %fusion.3), kind=kLoop, calls=%fused_computation.1 | loop fusion | flops 786432 | bytes 542720 | tf_op jit(solution)/shard_map/convert_element_type | solution.py:141
  11.2 12.4 %all-to-all-done.st_ref = bf16[16,8,2048]{2,1,0:T(8,128)(2,1)S(1)} async-done(((bf16[16,8,2048]{2,1,0:T(8,128)(2,1)}), bf16[16,8,2048]{2,1,0:T(8,128)(2,1)S(1)}, u32[]{:S(2)}, u32[]{:S(2)}) %all-to-all-start) | async-done | bytes 524320 | tf_op jit(solution)/shard_map/all_to_all | solution.py:137
  23.7 0.0 copy-done
  23.7 3.7 %shard_map.38 = f32[15,1,128]{2,1,0:T(1,128)} custom-call(s32[64,2]{1,0:T(8,128)S(1)} %copy.4.pairs_s.pairs_v, s32[64,2]{1,0:T(8,128)S(1)} %copy.4.pairs_s.pairs_v, bf16[16,8,2048]{2,1,0:T(8,128)(2,1)S(1)} %all-to-all-done.st_ref, bf16[15,64]{1,0:T(8,128)(2,1)S(1)} %copy-done, bf16[2048,128]{1,0:T(8,128)(2,1)S(1)} %fusion.window_ref), custom_call_target="tpu_custom_call" | custom-call | tf_op jit(solution)/shard_map/pallas_call | solution.py:142
  (2 shorter events, 0.0 us)
Async XLA Ops:
  2.0 7.4 %copy-start.1 = (s32[64,2]{0,1:T(2,128)S(1)}, s32[64,2]{0,1:T(2,128)}, u32[]{:S(2)}) copy-start(s32[64,2]{0,1:T(2,128)} %param.4) | copy-start | bytes 1540
  2.0 21.7 %all-to-all-start = ((bf16[16,8,2048]{2,1,0:T(8,128)(2,1)}), bf16[16,8,2048]{2,1,0:T(8,128)(2,1)S(1)}, u32[]{:S(2)}, u32[]{:S(2)}) async-start(bf16[16,8,2048]{2,1,0:T(8,128)(2,1)} %shard_map.37), calls=%async_computation | async-start | bytes 1048576 | tf_op jit(solution)/shard_map/all_to_all | solution.py:137
  9.5 14.1 %copy-start = (bf16[15,64]{1,0:T(8,128)(2,1)S(1)}, bf16[15,64]{1,0:T(8,128)(2,1)}, u32[]{:S(2)}) copy-start(bf16[15,64]{1,0:T(8,128)(2,1)} %inv_ref.1) | copy-start | bytes 5764

commit v12 on v11

--- a/solution.py
+++ b/solution.py
@@ -103,8 +103,9 @@
         out_ref[s] = series[s:s + 1, :]
 
 
-def regroup_kernel(in_hbm, out_ref, in_ref, sems):
-    n_chunk = out_ref.shape[0]
+def regroup_kernel(in_hbm, out_a, out_b, in_ref, sems):
+    n_chunk = out_a.shape[0]
+    width = out_a.shape[-1]
     half = n_chunk // 2
     rows_half = half * LOOK_R
     copies = []
@@ -118,7 +119,9 @@
         for q in range(2):
             copies[2 * k + q].wait()
             for c in range(q * half, (q + 1) * half):
-                out_ref[c, k * LOOK_R:(k + 1) * LOOK_R, :] = in_ref[k, c * LOOK_R:(c + 1) * LOOK_R, :]
+                block = in_ref[k, c * LOOK_R:(c + 1) * LOOK_R, :]
+                out_a[c, k * LOOK_R:(k + 1) * LOOK_R, :] = block[:, 0:width]
+                out_b[c, k * LOOK_R:(k + 1) * LOOK_R, :] = block[:, width:2 * width]
 
 
 def per_device(slc, pairs, inverse):
@@ -127,19 +130,20 @@
     steps = inverse.shape[0]
     _, _, all_rows, cols = slc.shape
     rows = all_rows // n_date
-    chunks = pl.pallas_call(
+    width = cols // 2
+    halves = pl.pallas_call(
         regroup_kernel,
-        out_shape=jax.ShapeDtypeStruct((n_date, 2 * rows, cols), slc.dtype),
+        out_shape=[jax.ShapeDtypeStruct((n_date, 2 * rows, width), slc.dtype)] * 2,
         in_specs=[pl.BlockSpec(memory_space=pl.ANY)],
-        out_specs=pl.BlockSpec(memory_space=pltpu.VMEM),
+        out_specs=[pl.BlockSpec(memory_space=pltpu.VMEM)] * 2,
         scratch_shapes=[pltpu.VMEM(slc.shape[1:], slc.dtype), pltpu.SemaphoreType.DMA((4,))],
     )(slc[0])
-    stripes = lax.all_to_all(chunks, "date", split_axis=0, concat_axis=0, tiled=True)
+    stripes = [lax.all_to_all(h, "date", split_axis=0, concat_axis=0, tiled=True) for h in halves]
     assert rows == LOOK_R and n_date % 8 == 0 and n_pair % 8 == 0
-    looks = cols // LOOK_C
-    col = lax.broadcasted_iota(jnp.int32, (cols, looks), 0) // LOOK_C
-    window = (col == lax.broadcasted_iota(jnp.int32, (cols, looks), 1)).astype(jnp.bfloat16)
-    out = pl.pallas_call(
+    looks = width // LOOK_C
+    col = lax.broadcasted_iota(jnp.int32, (width, looks), 0) // LOOK_C
+    window = (col == lax.broadcasted_iota(jnp.int32, (width, looks), 1)).astype(jnp.bfloat16)
+    outs = [pl.pallas_call(
         functools.partial(kernel, n_date, n_pair),
         out_shape=jax.ShapeDtypeStruct((steps, 1, looks), jnp.float32),
         in_specs=[
@@ -151,13 +155,13 @@
         ],
         out_specs=pl.BlockSpec(memory_space=pltpu.VMEM),
         scratch_shapes=[
-            pltpu.VMEM((n_date, 2 * LOOK_R, cols), jnp.float32),
-            pltpu.VMEM((n_date, 2 * LOOK_R, cols), jnp.float32),
-            pltpu.VMEM((n_pair + n_date, cols), jnp.float32),
+            pltpu.VMEM((n_date, 2 * LOOK_R, width), jnp.float32),
+            pltpu.VMEM((n_date, 2 * LOOK_R, width), jnp.float32),
+            pltpu.VMEM((n_pair + n_date, width), jnp.float32),
         ],
         compiler_params=pltpu.CompilerParams(vmem_limit_bytes=24 * 1024 * 1024),
-    )(pairs, pairs, stripes, inverse, window)
-    return out
+    )(pairs, pairs, st, inverse, window) for st in stripes]
+    return jnp.concatenate(outs, axis=2)
 
 
 def solution(mesh):

time: 27.6 us -> 36.6 us (1.33)
  blocking collectives: 0 us -> 17.4 us
  waiting for transfers between devices: 12.4 us -> 6.52 us
  starting transfers between devices: 7.43 us -> 3.66 us
  Pallas kernels: 5.63 us -> 6.81 us
    all_to_all x0 -> x1, blocking collectives: none -> 17.4 us  [per_device(): lax.all_to_all(h, 'date', split_axis=0, concat_axis=0, tiled=True)]
    all_to_all x1, waiting for transfers between devices: 12.4 us -> 6.52 us  [per_device(): lax.all_to_all(h, 'date', split_axis=0, concat_axis=0, tiled=True)]
    all_to_all x1, starting transfers between devices: 7.43 us -> 3.66 us  [per_device(): lax.all_to_all(h, 'date', split_axis=0, concat_axis=0, tiled=True)]
    pallas_call x1 -> x2, Pallas kernels: 3.68 us -> 4.87 us  [per_device(): pl.pallas_call(functools.partial(kernel, n_date, n_pair), out_shape=jax.S...]
    convert_element_type x1, other arithmetic: 1.7 us -> 0.87 us  [per_device(): (col == lax.broadcasted_iota(jnp.int32, (width, looks), 1)).astype(jnp.bf...]
    concatenate x0 -> x1, other arithmetic: none -> 0.7 us  [per_device(): return jnp.concatenate(outs, axis=2)]
  transfers between devices with their start and end apart: 1 -> 1, of which waited for: 1 -> 1; matrix products, arithmetic and copies ran while one was open for 7% -> 3% of each run, Pallas kernels for 0% -> 7%
where the time goes in v12:
time: 36.6 us; the launch traced here: 36.2 us
  blocking collectives  17.4 us (48%)
  Pallas kernels  6.81 us (19%)
  waiting for transfers between devices  6.52 us (18%)
  starting transfers between devices  3.66 us (10%)
  other arithmetic  1.57 us (4%)
    all_to_all x1, blocking collectives, per_device(): lax.all_to_all(h, 'date', split_axis=0, concat_axis=0, tiled=True)  17.4 us
    all_to_all x1, waiting for transfers between devices, per_device(): lax.all_to_all(h, 'date', split_axis=0, concat_axis=0, tiled=True)  6.52 us
    pallas_call x2, Pallas kernels, per_device(): pl.pallas_call(functools.partial(kernel, n_date, n_pair), out_shape=jax.S...  4.87 us
    all_to_all x1, starting transfers between devices, per_device(): lax.all_to_all(h, 'date', split_axis=0, concat_axis=0, tiled=True)  3.66 us
    pallas_call x1, Pallas kernels, per_device(): pl.pallas_call(regroup_kernel, out_shape=[jax.ShapeDtypeStruct((n_date, 2...  1.94 us
    convert_element_type x1, other arithmetic, per_device(): (col == lax.broadcasted_iota(jnp.int32, (width, looks), 1)).astype(jnp.bf...  0.87 us
  transfers between devices with their start and end apart: 1, of which 1 were waited for; matrix products, arithmetic and copies ran while one was open for 3% of the time, Pallas kernels for 7%

profile of v12, /device:TPU:0, one launch (start us, length us, event | category | flops | bytes accessed | tf_op | source)
XLA Modules:
  0.0 36.2 jit_solution(4286501294361235630)
XLA Ops:
  0.0 1.9 %shard_map.37 = (bf16[16,8,1024]{2,1,0:T(8,128)(2,1)}, bf16[16,8,1024]{2,1,0:T(8,128)(2,1)}) custom-call(bf16[2,64,2048]{2,1,0:T(8,128)(2,1)} %bitcast.1), custom_call_target="tpu_custom_call" | custom-call | tf_op jit(solution)/shard_map/pallas_call | solution.py:134
  1.9 17.4 %all_to_all.10.st_ref = bf16[16,8,1024]{2,1,0:T(8,128)(2,1)S(1)} all-to-all(bf16[16,8,1024]{2,1,0:T(8,128)(2,1)} %get-tuple-element.8), channel_id=1, replica_groups=mesh['grp'=2,'date'=16] {'date'}, dimensions={0} | all-to-all | bytes 524288 | tf_op jit(solution)/shard_map/all_to_all | solution.py:141
  19.4 0.0 copy-start.1
  19.4 3.7 %all-to-all-start = ((bf16[16,8,1024]{2,1,0:T(8,128)(2,1)}), bf16[16,8,1024]{2,1,0:T(8,128)(2,1)S(1)}, u32[]{:S(2)}, u32[]{:S(2)}) async-start(bf16[16,8,1024]{2,1,0:T(8,128)(2,1)} %get-tuple-element.7), calls=%async_computation | async-start | bytes 524288 | tf_op jit(solution)/shard_map/all_to_all | solution.py:141
  23.1 0.0 copy-done.1
  23.1 0.1 copy.4.pairs_s.pairs_v
  23.2 0.0 copy-start
  23.2 0.9 %fusion.window_ref = bf16[1024,64]{1,0:T(8,128)(2,1)S(1)} fusion(s32[1024]{0:T(1024)S(1)} %get-tuple-element.9, s32[1024]{0:T(1024)S(1)} %get-tuple-element.10, pred[1024]{0:T(1024)(128)(4,1)S(1)} %fusion.3), kind=kLoop, calls=%fused_computation.1 | loop fusion | flops 196608 | bytes 140288 | tf_op jit(solution)/shard_map/convert_element_type | solution.py:145
  24.1 0.0 copy-done
  24.1 2.4 %shard_map.39 = f32[15,1,64]{2,1,0:T(1,128)S(1)} custom-call(s32[64,2]{1,0:T(8,128)S(1)} %copy.4.pairs_s.pairs_v, s32[64,2]{1,0:T(8,128)S(1)} %copy.4.pairs_s.pairs_v, bf16[16,8,1024]{2,1,0:T(8,128)(2,1)S(1)} %all_to_all.10.st_ref, bf16[15,64]{1,0:T(8,128)(2,1)S(1)} %copy-done, bf16[1024,64]{1,0:T(8,128)(2,1)S(1)} %fusion.window_ref), custom_call_target="tpu_custom_call" | custom-call | tf_op jit(solution)/shard_map/pallas_call | solution.py:146
  26.5 6.5 %all-to-all-done.st_ref = bf16[16,8,1024]{2,1,0:T(8,128)(2,1)S(1)} async-done(((bf16[16,8,1024]{2,1,0:T(8,128)(2,1)}), bf16[16,8,1024]{2,1,0:T(8,128)(2,1)S(1)}, u32[]{:S(2)}, u32[]{:S(2)}) %all-to-all-start) | async-done | bytes 262176 | tf_op jit(solution)/shard_map/all_to_all | solution.py:141
  33.0 2.4 %shard_map.38 = f32[15,1,64]{2,1,0:T(1,128)S(1)} custom-call(s32[64,2]{1,0:T(8,128)S(1)} %copy.4.pairs_s.pairs_v, s32[64,2]{1,0:T(8,128)S(1)} %copy.4.pairs_s.pairs_v, bf16[16,8,1024]{2,1,0:T(8,128)(2,1)S(1)} %all-to-all-done.st_ref, bf16[15,64]{1,0:T(8,128)(2,1)S(1)} %copy-done, bf16[1024,64]{1,0:T(8,128)(2,1)S(1)} %fusion.window_ref), custom_call_target="tpu_custom_call" | custom-call | tf_op jit(solution)/shard_map/pallas_call | solution.py:146
  35.5 0.7 %pad_maximum_fusion = f32[15,1,128]{2,1,0:T(1,128)} fusion(f32[15,1,64]{2,1,0:T(1,128)S(1)} %shard_map.39, f32[15,1,64]{2,1,0:T(1,128)S(1)} %shard_map.38), kind=kLoop, calls=%fused_computation.5 | loop fusion | flops 1920 | bytes 15360 | tf_op jit(solution)/shard_map/concatenate | solution.py:164
  (2 shorter events, 0.0 us)
Async XLA Ops:
  19.4 3.7 %copy-start.1 = (s32[64,2]{0,1:T(2,128)S(1)}, s32[64,2]{0,1:T(2,128)}, u32[]{:S(2)}) copy-start(s32[64,2]{0,1:T(2,128)} %param.4) | copy-start | bytes 1540
  19.4 13.6 %all-to-all-start = ((bf16[16,8,1024]{2,1,0:T(8,128)(2,1)}), bf16[16,8,1024]{2,1,0:T(8,128)(2,1)S(1)}, u32[]{:S(2)}, u32[]{:S(2)}) async-start(bf16[16,8,1024]{2,1,0:T(8,128)(2,1)} %get-tuple-element.7), calls=%async_computation | async-start | bytes 524288 | tf_op jit(solution)/shard_map/all_to_all | solution.py:141
  23.2 0.9 %copy-start = (bf16[15,64]{1,0:T(8,128)(2,1)S(1)}, bf16[15,64]{1,0:T(8,128)(2,1)}, u32[]{:S(2)}) copy-start(bf16[15,64]{1,0:T(8,128)(2,1)} %inv_ref.3) | copy-start | bytes 5764

commit v13 on v11

--- a/solution.py
+++ b/solution.py
@@ -103,22 +103,29 @@
         out_ref[s] = series[s:s + 1, :]
 
 
-def regroup_kernel(in_hbm, out_ref, in_ref, sems):
+def regroup_kernel(in_hbm, out_hbm, in_ref, out_ref, sems, out_sems):
     n_chunk = out_ref.shape[0]
     half = n_chunk // 2
     rows_half = half * LOOK_R
-    copies = []
-    for k in range(2):
-        for q in range(2):
+    copies = {}
+    for q in range(2):
+        for k in range(2):
             rows = pl.ds(q * rows_half, rows_half)
-            copy = pltpu.make_async_copy(in_hbm.at[k, rows], in_ref.at[k, rows], sems.at[2 * k + q])
+            copy = pltpu.make_async_copy(in_hbm.at[k, rows], in_ref.at[k, rows], sems.at[2 * q + k])
             copy.start()
-            copies.append(copy)
-    for k in range(2):
-        for q in range(2):
-            copies[2 * k + q].wait()
+            copies[q, k] = copy
+    outs = []
+    for q in range(2):
+        for k in range(2):
+            copies[q, k].wait()
             for c in range(q * half, (q + 1) * half):
                 out_ref[c, k * LOOK_R:(k + 1) * LOOK_R, :] = in_ref[k, c * LOOK_R:(c + 1) * LOOK_R, :]
+        chunk = pl.ds(q * half, half)
+        out = pltpu.make_async_copy(out_ref.at[chunk], out_hbm.at[chunk], out_sems.at[q])
+        out.start()
+        outs.append(out)
+    for out in outs:
+        out.wait()
 
 
 def per_device(slc, pairs, inverse):
@@ -131,8 +138,13 @@
         regroup_kernel,
         out_shape=jax.ShapeDtypeStruct((n_date, 2 * rows, cols), slc.dtype),
         in_specs=[pl.BlockSpec(memory_space=pl.ANY)],
-        out_specs=pl.BlockSpec(memory_space=pltpu.VMEM),
-        scratch_shapes=[pltpu.VMEM(slc.shape[1:], slc.dtype), pltpu.SemaphoreType.DMA((4,))],
+        out_specs=pl.BlockSpec(memory_space=pl.ANY),
+        scratch_shapes=[
+            pltpu.VMEM(slc.shape[1:], slc.dtype),
+            pltpu.VMEM((n_date, 2 * rows, cols), slc.dtype),
+            pltpu.SemaphoreType.DMA((4,)),
+            pltpu.SemaphoreType.DMA((2,)),
+        ],
     )(slc[0])
     stripes = lax.all_to_all(chunks, "date", split_axis=0, concat_axis=0, tiled=True)
     assert rows == LOOK_R and n_date % 8 == 0 and n_pair % 8 == 0

time: 27.6 us -> 27.5 us (level)
  no operation moved by 1% of the time
where the time goes in v13:
time: 27.5 us; the launch traced here: 27.3 us
  waiting for transfers between devices  12.4 us (45%)
  starting transfers between devices  7.43 us (27%)
  Pallas kernels  5.55 us (20%)
  other arithmetic  1.71 us (6%)
    all_to_all x1, waiting for transfers between devices, per_device(): lax.all_to_all(chunks, 'date', split_axis=0, concat_axis=0, tiled=True)  12.4 us
    all_to_all x1, starting transfers between devices, per_device(): lax.all_to_all(chunks, 'date', split_axis=0, concat_axis=0, tiled=True)  7.43 us
    pallas_call x1, Pallas kernels, per_device(): pl.pallas_call(functools.partial(kernel, n_date, n_pair), out_shape=jax.S...  3.68 us
    pallas_call x1, Pallas kernels, per_device(): pl.pallas_call(regroup_kernel, out_shape=jax.ShapeDtypeStruct((n_date, 2...  1.87 us
    convert_element_type x1, other arithmetic, per_device(): (col == lax.broadcasted_iota(jnp.int32, (cols, looks), 1)).astype(jnp.bfl...  1.7 us
  transfers between devices with their start and end apart: 1, of which 1 were waited for; matrix products, arithmetic and copies ran while one was open for 7% of the time, Pallas kernels for 0%

profile of v13, /device:TPU:0, one launch (start us, length us, event | category | flops | bytes accessed | tf_op | source)
XLA Modules:
  0.0 27.3 jit_solution(15891136733767444863)
XLA Ops:
  0.0 1.9 %shard_map.37 = bf16[16,8,2048]{2,1,0:T(8,128)(2,1)} custom-call(bf16[2,64,2048]{2,1,0:T(8,128)(2,1)} %bitcast.1), custom_call_target="tpu_custom_call" | custom-call | tf_op jit(solution)/shard_map/pallas_call | solution.py:137
  1.9 0.0 copy-start.1
  1.9 7.4 %all-to-all-start = ((bf16[16,8,2048]{2,1,0:T(8,128)(2,1)}), bf16[16,8,2048]{2,1,0:T(8,128)(2,1)S(1)}, u32[]{:S(2)}, u32[]{:S(2)}) async-start(bf16[16,8,2048]{2,1,0:T(8,128)(2,1)} %shard_map.37), calls=%async_computation | async-start | bytes 1048576 | tf_op jit(solution)/shard_map/all_to_all | solution.py:149
  9.3 0.0 copy-done.1
  9.3 0.1 copy.4.pairs_s.pairs_v
  9.4 0.0 copy-start
  9.5 1.7 %fusion.window_ref = bf16[2048,128]{1,0:T(8,128)(2,1)S(1)} fusion(s32[2048]{0:T(1024)S(1)} %get-tuple-element.5, s32[2048]{0:T(1024)S(1)} %get-tuple-element.6, pred[2048]{0:T(1024)(128)(4,1)S(1)} %fusion.3), kind=kLoop, calls=%fused_computation.1 | loop fusion | flops 786432 | bytes 542720 | tf_op jit(solution)/shard_map/convert_element_type | solution.py:153
  11.2 12.4 %all-to-all-done.st_ref = bf16[16,8,2048]{2,1,0:T(8,128)(2,1)S(1)} async-done(((bf16[16,8,2048]{2,1,0:T(8,128)(2,1)}), bf16[16,8,2048]{2,1,0:T(8,128)(2,1)S(1)}, u32[]{:S(2)}, u32[]{:S(2)}) %all-to-all-start) | async-done | bytes 524320 | tf_op jit(solution)/shard_map/all_to_all | solution.py:149
  23.6 0.0 copy-done
  23.6 3.7 %shard_map.38 = f32[15,1,128]{2,1,0:T(1,128)} custom-call(s32[64,2]{1,0:T(8,128)S(1)} %copy.4.pairs_s.pairs_v, s32[64,2]{1,0:T(8,128)S(1)} %copy.4.pairs_s.pairs_v, bf16[16,8,2048]{2,1,0:T(8,128)(2,1)S(1)} %all-to-all-done.st_ref, bf16[15,64]{1,0:T(8,128)(2,1)S(1)} %copy-done, bf16[2048,128]{1,0:T(8,128)(2,1)S(1)} %fusion.window_ref), custom_call_target="tpu_custom_call" | custom-call | tf_op jit(solution)/shard_map/pallas_call | solution.py:154
  (2 shorter events, 0.0 us)
Async XLA Ops:
  1.9 7.4 %copy-start.1 = (s32[64,2]{0,1:T(2,128)S(1)}, s32[64,2]{0,1:T(2,128)}, u32[]{:S(2)}) copy-start(s32[64,2]{0,1:T(2,128)} %param.4) | copy-start | bytes 1540
  1.9 21.7 %all-to-all-start = ((bf16[16,8,2048]{2,1,0:T(8,128)(2,1)}), bf16[16,8,2048]{2,1,0:T(8,128)(2,1)S(1)}, u32[]{:S(2)}, u32[]{:S(2)}) async-start(bf16[16,8,2048]{2,1,0:T(8,128)(2,1)} %shard_map.37), calls=%async_computation | async-start | bytes 1048576 | tf_op jit(solution)/shard_map/all_to_all | solution.py:149
  9.4 14.1 %copy-start = (bf16[15,64]{1,0:T(8,128)(2,1)S(1)}, bf16[15,64]{1,0:T(8,128)(2,1)}, u32[]{:S(2)}) copy-start(bf16[15,64]{1,0:T(8,128)(2,1)} %inv_ref.1) | copy-start | bytes 5764

commit v14 on v11

--- a/solution.py
+++ b/solution.py
@@ -34,31 +34,24 @@
     cols = st_ref.shape[-1]
     looks = cols // LOOK_C
 
+    sub = lax.broadcasted_iota(jnp.int32, (2 * LOOK_R, cols), 0)
+    sign = jnp.where(sub < LOOK_R, -1.0, 1.0).astype(jnp.float32)
+
     def date_body(d, carry):
-        f_ref[d] = st_ref[d].astype(jnp.float32)
+        x = st_ref[d].astype(jnp.float32)
+        f_ref[d] = x
+        g_ref[d] = pltpu.roll(x, LOOK_R, 0) * sign
         return carry
 
     lax.fori_loop(0, n_date, date_body, 0)
-
-    sub = lax.broadcasted_iota(jnp.int32, (2 * LOOK_R, cols), 0)
-    sign = jnp.where(sub < LOOK_R, -1.0, 1.0).astype(jnp.float32)
-
-    def swap_body(d, carry):
-        g_ref[d] = pltpu.roll(f_ref[d], LOOK_R, 0) * sign
-        return carry
-
-    lax.fori_loop(0, n_date, swap_body, 0)
 
     masks = {h: (sub & h) == 0 for h in (4, 2, 1)}
 
     def combine(x, y, h):
         m = masks[h]
-        w = jnp.where(m, y, x)
         if h == 4:
-            moved = pltpu.roll(w, 4, 0)
-        else:
-            moved = jnp.where(m, pltpu.roll(w, 8 - h, 0), pltpu.roll(w, h, 0))
-        return jnp.where(m, x, y) + moved
+            return jnp.where(m, x, y) + pltpu.roll(jnp.where(m, y, x), 4, 0)
+        return jnp.where(m, x + pltpu.roll(x, 8 - h, 0), y + pltpu.roll(y, h, 0))
 
     def power_body(g, carry):
         level = []

time: 27.6 us -> 27.4 us (level)
  no operation moved by 1% of the time
where the time goes in v14:
time: 27.4 us; the launch traced here: 27.2 us
  waiting for transfers between devices  12.4 us (45%)
  starting transfers between devices  7.43 us (27%)
  Pallas kernels  5.47 us (20%)
  other arithmetic  1.71 us (6%)
    all_to_all x1, waiting for transfers between devices, per_device(): lax.all_to_all(chunks, 'date', split_axis=0, concat_axis=0, tiled=True)  12.4 us
    all_to_all x1, starting transfers between devices, per_device(): lax.all_to_all(chunks, 'date', split_axis=0, concat_axis=0, tiled=True)  7.43 us
    pallas_call x1, Pallas kernels, per_device(): pl.pallas_call(functools.partial(kernel, n_date, n_pair), out_shape=jax.S...  3.52 us
    pallas_call x1, Pallas kernels, per_device(): pl.pallas_call(regroup_kernel, out_shape=jax.ShapeDtypeStruct((n_date, 2...  1.95 us
    convert_element_type x1, other arithmetic, per_device(): (col == lax.broadcasted_iota(jnp.int32, (cols, looks), 1)).astype(jnp.bfl...  1.7 us
  transfers between devices with their start and end apart: 1, of which 1 were waited for; matrix products, arithmetic and copies ran while one was open for 7% of the time, Pallas kernels for 0%

profile of v14, /device:TPU:0, one launch (start us, length us, event | category | flops | bytes accessed | tf_op | source)
XLA Modules:
  0.0 27.2 jit_solution(10340425670625894960)
XLA Ops:
  0.0 1.9 %shard_map.37 = bf16[16,8,2048]{2,1,0:T(8,128)(2,1)} custom-call(bf16[2,64,2048]{2,1,0:T(8,128)(2,1)} %bitcast.1), custom_call_target="tpu_custom_call" | custom-call | tf_op jit(solution)/shard_map/pallas_call | solution.py:123
  2.0 0.0 copy-start.1
  2.0 7.4 %all-to-all-start = ((bf16[16,8,2048]{2,1,0:T(8,128)(2,1)}), bf16[16,8,2048]{2,1,0:T(8,128)(2,1)S(1)}, u32[]{:S(2)}, u32[]{:S(2)}) async-start(bf16[16,8,2048]{2,1,0:T(8,128)(2,1)} %shard_map.37), calls=%async_computation | async-start | bytes 1048576 | tf_op jit(solution)/shard_map/all_to_all | solution.py:130
  9.4 0.0 copy-done.1
  9.4 0.1 copy.4.pairs_s.pairs_v
  9.5 0.0 copy-start
  9.5 1.7 %fusion.window_ref = bf16[2048,128]{1,0:T(8,128)(2,1)S(1)} fusion(s32[2048]{0:T(1024)S(1)} %get-tuple-element.5, s32[2048]{0:T(1024)S(1)} %get-tuple-element.6, pred[2048]{0:T(1024)(128)(4,1)S(1)} %fusion.3), kind=kLoop, calls=%fused_computation.1 | loop fusion | flops 786432 | bytes 542720 | tf_op jit(solution)/shard_map/convert_element_type | solution.py:134
  11.2 12.4 %all-to-all-done.st_ref = bf16[16,8,2048]{2,1,0:T(8,128)(2,1)S(1)} async-done(((bf16[16,8,2048]{2,1,0:T(8,128)(2,1)}), bf16[16,8,2048]{2,1,0:T(8,128)(2,1)S(1)}, u32[]{:S(2)}, u32[]{:S(2)}) %all-to-all-start) | async-done | bytes 524320 | tf_op jit(solution)/shard_map/all_to_all | solution.py:130
  23.7 0.0 copy-done
  23.7 3.5 %shard_map.38 = f32[15,1,128]{2,1,0:T(1,128)} custom-call(s32[64,2]{1,0:T(8,128)S(1)} %copy.4.pairs_s.pairs_v, s32[64,2]{1,0:T(8,128)S(1)} %copy.4.pairs_s.pairs_v, bf16[16,8,2048]{2,1,0:T(8,128)(2,1)S(1)} %all-to-all-done.st_ref, bf16[15,64]{1,0:T(8,128)(2,1)S(1)} %copy-done, bf16[2048,128]{1,0:T(8,128)(2,1)S(1)} %fusion.window_ref), custom_call_target="tpu_custom_call" | custom-call | tf_op jit(solution)/shard_map/pallas_call | solution.py:135
  (2 shorter events, 0.0 us)
Async XLA Ops:
  2.0 7.4 %copy-start.1 = (s32[64,2]{0,1:T(2,128)S(1)}, s32[64,2]{0,1:T(2,128)}, u32[]{:S(2)}) copy-start(s32[64,2]{0,1:T(2,128)} %param.4) | copy-start | bytes 1540
  2.0 21.7 %all-to-all-start = ((bf16[16,8,2048]{2,1,0:T(8,128)(2,1)}), bf16[16,8,2048]{2,1,0:T(8,128)(2,1)S(1)}, u32[]{:S(2)}, u32[]{:S(2)}) async-start(bf16[16,8,2048]{2,1,0:T(8,128)(2,1)} %shard_map.37), calls=%async_computation | async-start | bytes 1048576 | tf_op jit(solution)/shard_map/all_to_all | solution.py:130
  9.5 14.1 %copy-start = (bf16[15,64]{1,0:T(8,128)(2,1)S(1)}, bf16[15,64]{1,0:T(8,128)(2,1)}, u32[]{:S(2)}) copy-start(bf16[15,64]{1,0:T(8,128)(2,1)} %inv_ref.1) | copy-start | bytes 5764

commit v15 on v14

--- a/solution.py
+++ b/solution.py
@@ -30,7 +30,7 @@
     return out
 
 
-def kernel(n_date, n_pair, pairs_s, pairs_v, st_ref, inv_ref, window_ref, out_ref, f_ref, g_ref, rows_ref):
+def kernel(n_date, n_pair, pairs_s, pairs_v, st_ref, inv_ref, window_ref, out_ref, f_ref, g_ref, rows_ref, lp_ref, proxy_ref):
     cols = st_ref.shape[-1]
     looks = cols // LOOK_C
 
@@ -80,17 +80,27 @@
     lax.fori_loop(0, n_pair // 8, pair_body, 0)
 
     looked = dot3(split3(rows_ref[...]), window_ref[...], True)
-    looked_cross = looked[0:n_pair]
     looked_pow = looked[n_pair:n_pair + n_date]
+    rows_ref[0:n_pair, 0:looks] = looked[0:n_pair]
 
-    date_idx = lax.broadcasted_iota(jnp.int32, (n_pair, n_date), 1)
-    sel_a = (pairs_v[:, 0:1] == date_idx).astype(jnp.bfloat16)
-    sel_b = (pairs_v[:, 1:2] == date_idx).astype(jnp.bfloat16)
-    pow_parts = split3(looked_pow)
-    looked_ref = dot3(pow_parts, sel_a, False)
-    looked_sec = dot3(pow_parts, sel_b, False)
+    for d in range(n_date):
+        lp_ref[d] = jnp.broadcast_to(looked_pow[d:d + 1, :], (8, looks))
+    lp_sub = lax.broadcasted_iota(jnp.int32, (8, looks), 0)
 
-    proxy = looked_cross / jnp.sqrt(looked_ref * looked_sec + 1e-06)
+    def proxy_body(g, carry):
+        ref_pow = jnp.zeros((8, looks), jnp.float32)
+        sec_pow = jnp.zeros((8, looks), jnp.float32)
+        for i in range(8):
+            p = g * 8 + i
+            ref_pow = jnp.where(lp_sub == i, lp_ref[pairs_s[p, 0]], ref_pow)
+            sec_pow = jnp.where(lp_sub == i, lp_ref[pairs_s[p, 1]], sec_pow)
+        start = pl.multiple_of(g * 8, 8)
+        cross = rows_ref[pl.ds(start, 8), 0:looks]
+        proxy_ref[pl.ds(start, 8), :] = cross / jnp.sqrt(ref_pow * sec_pow + 1e-06)
+        return carry
+
+    lax.fori_loop(0, n_pair // 8, proxy_body, 0)
+    proxy = proxy_ref[...]
     series = dot3(split3(proxy), inv_ref[...], False)
     for s in range(series.shape[0]):
         out_ref[s] = series[s:s + 1, :]
@@ -147,6 +157,8 @@
             pltpu.VMEM((n_date, 2 * LOOK_R, cols), jnp.float32),
             pltpu.VMEM((n_date, 2 * LOOK_R, cols), jnp.float32),
             pltpu.VMEM((n_pair + n_date, cols), jnp.float32),
+            pltpu.VMEM((n_date, 8, looks), jnp.float32),
+            pltpu.VMEM((n_pair, looks), jnp.float32),
         ],
         compiler_params=pltpu.CompilerParams(vmem_limit_bytes=24 * 1024 * 1024),
     )(pairs, pairs, stripes, inverse, window)

time: 27.4 us -> 27.5 us (level)
  no operation moved by 1% of the time
where the time goes in v15:
time: 27.5 us; the launch traced here: 27.3 us
  waiting for transfers between devices  12.4 us (45%)
  starting transfers between devices  7.43 us (27%)
  Pallas kernels  5.56 us (20%)
  other arithmetic  1.71 us (6%)
    all_to_all x1, waiting for transfers between devices, per_device(): lax.all_to_all(chunks, 'date', split_axis=0, concat_axis=0, tiled=True)  12.4 us
    all_to_all x1, starting transfers between devices, per_device(): lax.all_to_all(chunks, 'date', split_axis=0, concat_axis=0, tiled=True)  7.43 us
    pallas_call x1, Pallas kernels, per_device(): pl.pallas_call(functools.partial(kernel, n_date, n_pair), out_shape=jax.S...  3.61 us
    pallas_call x1, Pallas kernels, per_device(): pl.pallas_call(regroup_kernel, out_shape=jax.ShapeDtypeStruct((n_date, 2...  1.95 us
    convert_element_type x1, other arithmetic, per_device(): (col == lax.broadcasted_iota(jnp.int32, (cols, looks), 1)).astype(jnp.bfl...  1.7 us
  transfers between devices with their start and end apart: 1, of which 1 were waited for; matrix products, arithmetic and copies ran while one was open for 7% of the time, Pallas kernels for 0%

profile of v15, /device:TPU:0, one launch (start us, length us, event | category | flops | bytes accessed | tf_op | source)
XLA Modules:
  0.0 27.3 jit_solution(12527445625370009111)
XLA Ops:
  0.0 1.9 %shard_map.37 = bf16[16,8,2048]{2,1,0:T(8,128)(2,1)} custom-call(bf16[2,64,2048]{2,1,0:T(8,128)(2,1)} %bitcast.1), custom_call_target="tpu_custom_call" | custom-call | tf_op jit(solution)/shard_map/pallas_call | solution.py:133
  2.0 0.0 copy-start.1
  2.0 7.4 %all-to-all-start = ((bf16[16,8,2048]{2,1,0:T(8,128)(2,1)}), bf16[16,8,2048]{2,1,0:T(8,128)(2,1)S(1)}, u32[]{:S(2)}, u32[]{:S(2)}) async-start(bf16[16,8,2048]{2,1,0:T(8,128)(2,1)} %shard_map.37), calls=%async_computation | async-start | bytes 1048576 | tf_op jit(solution)/shard_map/all_to_all | solution.py:140
  9.4 0.0 copy-done.1
  9.4 0.1 copy.4.pairs_s.pairs_v
  9.5 0.0 copy-start
  9.5 1.7 %fusion.window_ref = bf16[2048,128]{1,0:T(8,128)(2,1)S(1)} fusion(s32[2048]{0:T(1024)S(1)} %get-tuple-element.5, s32[2048]{0:T(1024)S(1)} %get-tuple-element.6, pred[2048]{0:T(1024)(128)(4,1)S(1)} %fusion.3), kind=kLoop, calls=%fused_computation.1 | loop fusion | flops 786432 | bytes 542720 | tf_op jit(solution)/shard_map/convert_element_type | solution.py:144
  11.2 12.4 %all-to-all-done.st_ref = bf16[16,8,2048]{2,1,0:T(8,128)(2,1)S(1)} async-done(((bf16[16,8,2048]{2,1,0:T(8,128)(2,1)}), bf16[16,8,2048]{2,1,0:T(8,128)(2,1)S(1)}, u32[]{:S(2)}, u32[]{:S(2)}) %all-to-all-start) | async-done | bytes 524320 | tf_op jit(solution)/shard_map/all_to_all | solution.py:140
  23.7 0.0 copy-done
  23.7 3.6 %shard_map.38 = f32[15,1,128]{2,1,0:T(1,128)} custom-call(s32[64,2]{1,0:T(8,128)S(1)} %copy.4.pairs_s.pairs_v, s32[64,2]{1,0:T(8,128)S(1)} %copy.4.pairs_s.pairs_v, bf16[16,8,2048]{2,1,0:T(8,128)(2,1)S(1)} %all-to-all-done.st_ref, bf16[15,64]{1,0:T(8,128)(2,1)S(1)} %copy-done, bf16[2048,128]{1,0:T(8,128)(2,1)S(1)} %fusion.window_ref), custom_call_target="tpu_custom_call" | custom-call | tf_op jit(solution)/shard_map/pallas_call | solution.py:145
  (2 shorter events, 0.0 us)
Async XLA Ops:
  2.0 7.4 %copy-start.1 = (s32[64,2]{0,1:T(2,128)S(1)}, s32[64,2]{0,1:T(2,128)}, u32[]{:S(2)}) copy-start(s32[64,2]{0,1:T(2,128)} %param.4) | copy-start | bytes 1540
  2.0 21.7 %all-to-all-start = ((bf16[16,8,2048]{2,1,0:T(8,128)(2,1)}), bf16[16,8,2048]{2,1,0:T(8,128)(2,1)S(1)}, u32[]{:S(2)}, u32[]{:S(2)}) async-start(bf16[16,8,2048]{2,1,0:T(8,128)(2,1)} %shard_map.37), calls=%async_computation | async-start | bytes 1048576 | tf_op jit(solution)/shard_map/all_to_all | solution.py:140
  9.5 14.1 %copy-start = (bf16[15,64]{1,0:T(8,128)(2,1)S(1)}, bf16[15,64]{1,0:T(8,128)(2,1)}, u32[]{:S(2)}) copy-start(bf16[15,64]{1,0:T(8,128)(2,1)} %inv_ref.1) | copy-start | bytes 5764

commit v16 on v14

--- a/solution.py
+++ b/solution.py
@@ -30,7 +30,10 @@
     return out
 
 
-def kernel(n_date, n_pair, pairs_s, pairs_v, st_ref, inv_ref, window_ref, out_ref, f_ref, g_ref, rows_ref):
+def kernel(n_date, n_pair, pairs_any, pairs_v, st_ref, inv_ref, window_ref, out_ref, f_ref, g_ref, rows_ref,
+           pairs_s, pairs_sem):
+    pairs_copy = pltpu.make_async_copy(pairs_any, pairs_s, pairs_sem)
+    pairs_copy.start()
     cols = st_ref.shape[-1]
     looks = cols // LOOK_C
 
@@ -65,6 +68,8 @@
         return carry
 
     lax.fori_loop(0, n_date // 8, power_body, 0)
+
+    pairs_copy.wait()
 
     def pair_body(g, carry):
         level = []
@@ -136,7 +141,7 @@
         functools.partial(kernel, n_date, n_pair),
         out_shape=jax.ShapeDtypeStruct((steps, 1, looks), jnp.float32),
         in_specs=[
-            pl.BlockSpec(memory_space=pltpu.SMEM),
+            pl.BlockSpec(memory_space=pl.ANY),
             pl.BlockSpec(memory_space=pltpu.VMEM),
             pl.BlockSpec(memory_space=pltpu.VMEM),
             pl.BlockSpec(memory_space=pltpu.VMEM),
@@ -147,6 +152,8 @@
             pltpu.VMEM((n_date, 2 * LOOK_R, cols), jnp.float32),
             pltpu.VMEM((n_date, 2 * LOOK_R, cols), jnp.float32),
             pltpu.VMEM((n_pair + n_date, cols), jnp.float32),
+            pltpu.SMEM(pairs.shape, pairs.dtype),
+            pltpu.SemaphoreType.DMA(()),
         ],
         compiler_params=pltpu.CompilerParams(vmem_limit_bytes=24 * 1024 * 1024),
     )(pairs, pairs, stripes, inverse, window)

time: 27.4 us -> 27.1 us (0.989)
  Pallas kernels: 5.47 us -> 5.11 us
    pallas_call x1, Pallas kernels: 3.52 us -> 3.16 us  [per_device(): pl.pallas_call(functools.partial(kernel, n_date, n_pair), out_shape=jax.S...]
where the time goes in v16:
time: 27.1 us; the launch traced here: 26.8 us
  waiting for transfers between devices  12.4 us (46%)
  starting transfers between devices  7.43 us (27%)
  Pallas kernels  5.11 us (19%)
  other arithmetic  1.71 us (6%)
    all_to_all x1, waiting for transfers between devices, per_device(): lax.all_to_all(chunks, 'date', split_axis=0, concat_axis=0, tiled=True)  12.4 us
    all_to_all x1, starting transfers between devices, per_device(): lax.all_to_all(chunks, 'date', split_axis=0, concat_axis=0, tiled=True)  7.43 us
    pallas_call x1, Pallas kernels, per_device(): pl.pallas_call(functools.partial(kernel, n_date, n_pair), out_shape=jax.S...  3.16 us
    pallas_call x1, Pallas kernels, per_device(): pl.pallas_call(regroup_kernel, out_shape=jax.ShapeDtypeStruct((n_date, 2...  1.95 us
    convert_element_type x1, other arithmetic, per_device(): (col == lax.broadcasted_iota(jnp.int32, (cols, looks), 1)).astype(jnp.bfl...  1.7 us
  transfers between devices with their start and end apart: 1, of which 1 were waited for; matrix products, arithmetic and copies ran while one was open for 7% of the time, Pallas kernels for 0%

profile of v16, /device:TPU:0, one launch (start us, length us, event | category | flops | bytes accessed | tf_op | source)
XLA Modules:
  0.0 26.8 jit_solution(5172621518793874697)
XLA Ops:
  0.0 1.9 %shard_map.37 = bf16[16,8,2048]{2,1,0:T(8,128)(2,1)} custom-call(bf16[2,64,2048]{2,1,0:T(8,128)(2,1)} %bitcast.1), custom_call_target="tpu_custom_call" | custom-call | tf_op jit(solution)/shard_map/pallas_call | solution.py:128
  2.0 0.0 copy-start.1
  2.0 7.4 %all-to-all-start = ((bf16[16,8,2048]{2,1,0:T(8,128)(2,1)}), bf16[16,8,2048]{2,1,0:T(8,128)(2,1)S(1)}, u32[]{:S(2)}, u32[]{:S(2)}) async-start(bf16[16,8,2048]{2,1,0:T(8,128)(2,1)} %shard_map.37), calls=%async_computation | async-start | bytes 1048576 | tf_op jit(solution)/shard_map/all_to_all | solution.py:135
  9.4 0.0 copy-done.1
  9.4 0.1 copy.4.pairs_any.pairs_v
  9.5 0.0 copy-start
  9.5 1.7 %fusion.window_ref = bf16[2048,128]{1,0:T(8,128)(2,1)S(1)} fusion(s32[2048]{0:T(1024)S(1)} %get-tuple-element.5, s32[2048]{0:T(1024)S(1)} %get-tuple-element.6, pred[2048]{0:T(1024)(128)(4,1)S(1)} %fusion.3), kind=kLoop, calls=%fused_computation.1 | loop fusion | flops 786432 | bytes 542720 | tf_op jit(solution)/shard_map/convert_element_type | solution.py:139
  11.2 12.4 %all-to-all-done.st_ref = bf16[16,8,2048]{2,1,0:T(8,128)(2,1)S(1)} async-done(((bf16[16,8,2048]{2,1,0:T(8,128)(2,1)}), bf16[16,8,2048]{2,1,0:T(8,128)(2,1)S(1)}, u32[]{:S(2)}, u32[]{:S(2)}) %all-to-all-start) | async-done | bytes 524320 | tf_op jit(solution)/shard_map/all_to_all | solution.py:135
  23.7 0.0 copy-done
  23.7 3.2 %shard_map.38 = f32[15,1,128]{2,1,0:T(1,128)} custom-call(s32[64,2]{1,0:T(8,128)S(1)} %copy.4.pairs_any.pairs_v, s32[64,2]{1,0:T(8,128)S(1)} %copy.4.pairs_any.pairs_v, bf16[16,8,2048]{2,1,0:T(8,128)(2,1)S(1)} %all-to-all-done.st_ref, bf16[15,64]{1,0:T(8,128)(2,1)S(1)} %copy-done, bf16[2048,128]{1,0:T(8,128)(2,1)S(1)} %fusion.window_ref), custom_call_target="tpu_custom_call" | custom-call | tf_op jit(solution)/shard_map/pallas_call | solution.py:140
  (2 shorter events, 0.0 us)
Async XLA Ops:
  2.0 7.4 %copy-start.1 = (s32[64,2]{0,1:T(2,128)S(1)}, s32[64,2]{0,1:T(2,128)}, u32[]{:S(2)}) copy-start(s32[64,2]{0,1:T(2,128)} %param.4) | copy-start | bytes 1540
  2.0 21.7 %all-to-all-start = ((bf16[16,8,2048]{2,1,0:T(8,128)(2,1)}), bf16[16,8,2048]{2,1,0:T(8,128)(2,1)S(1)}, u32[]{:S(2)}, u32[]{:S(2)}) async-start(bf16[16,8,2048]{2,1,0:T(8,128)(2,1)} %shard_map.37), calls=%async_computation | async-start | bytes 1048576 | tf_op jit(solution)/shard_map/all_to_all | solution.py:135
  9.5 14.1 %copy-start = (bf16[15,64]{1,0:T(8,128)(2,1)S(1)}, bf16[15,64]{1,0:T(8,128)(2,1)}, u32[]{:S(2)}) copy-start(bf16[15,64]{1,0:T(8,128)(2,1)} %inv_ref.1) | copy-start | bytes 5764

commit v17 on v16

--- a/solution.py
+++ b/solution.py
@@ -84,16 +84,19 @@
 
     lax.fori_loop(0, n_pair // 8, pair_body, 0)
 
-    looked = dot3(split3(rows_ref[...]), window_ref[...], True)
+    n_rows = n_pair + n_date
+    stacked = jnp.concatenate(split3(rows_ref[...]), axis=0)
+    parts = jnp.dot(stacked, window_ref[...], preferred_element_type=jnp.float32)
+    looked = (parts[0:n_rows] + parts[n_rows:2 * n_rows]) + parts[2 * n_rows:3 * n_rows]
     looked_cross = looked[0:n_pair]
     looked_pow = looked[n_pair:n_pair + n_date]
 
     date_idx = lax.broadcasted_iota(jnp.int32, (n_pair, n_date), 1)
     sel_a = (pairs_v[:, 0:1] == date_idx).astype(jnp.bfloat16)
     sel_b = (pairs_v[:, 1:2] == date_idx).astype(jnp.bfloat16)
-    pow_parts = split3(looked_pow)
-    looked_ref = dot3(pow_parts, sel_a, False)
-    looked_sec = dot3(pow_parts, sel_b, False)
+    picked = dot3(split3(looked_pow), jnp.concatenate([sel_a, sel_b], axis=0), False)
+    looked_ref = picked[0:n_pair]
+    looked_sec = picked[n_pair:2 * n_pair]
 
     proxy = looked_cross / jnp.sqrt(looked_ref * looked_sec + 1e-06)
     series = dot3(split3(proxy), inv_ref[...], False)

time: 27.1 us -> 27.1 us (level)
  no operation moved by 1% of the time
where the time goes in v17:
time: 27.1 us; the launch traced here: 26.8 us
  waiting for transfers between devices  12.4 us (46%)
  starting transfers between devices  7.43 us (27%)
  Pallas kernels  5.1 us (19%)
  other arithmetic  1.71 us (6%)
    all_to_all x1, waiting for transfers between devices, per_device(): lax.all_to_all(chunks, 'date', split_axis=0, concat_axis=0, tiled=True)  12.4 us
    all_to_all x1, starting transfers between devices, per_device(): lax.all_to_all(chunks, 'date', split_axis=0, concat_axis=0, tiled=True)  7.43 us
    pallas_call x1, Pallas kernels, per_device(): pl.pallas_call(functools.partial(kernel, n_date, n_pair), out_shape=jax.S...  3.15 us
    pallas_call x1, Pallas kernels, per_device(): pl.pallas_call(regroup_kernel, out_shape=jax.ShapeDtypeStruct((n_date, 2...  1.95 us
    convert_element_type x1, other arithmetic, per_device(): (col == lax.broadcasted_iota(jnp.int32, (cols, looks), 1)).astype(jnp.bfl...  1.7 us
  transfers between devices with their start and end apart: 1, of which 1 were waited for; matrix products, arithmetic and copies ran while one was open for 7% of the time, Pallas kernels for 0%

profile of v17, /device:TPU:0, one launch (start us, length us, event | category | flops | bytes accessed | tf_op | source)
XLA Modules:
  0.0 26.8 jit_solution(6406508566338140685)
XLA Ops:
  0.0 1.9 %shard_map.37 = bf16[16,8,2048]{2,1,0:T(8,128)(2,1)} custom-call(bf16[2,64,2048]{2,1,0:T(8,128)(2,1)} %bitcast.1), custom_call_target="tpu_custom_call" | custom-call | tf_op jit(solution)/shard_map/pallas_call | solution.py:131
  2.0 0.0 copy-start.1
  2.0 7.4 %all-to-all-start = ((bf16[16,8,2048]{2,1,0:T(8,128)(2,1)}), bf16[16,8,2048]{2,1,0:T(8,128)(2,1)S(1)}, u32[]{:S(2)}, u32[]{:S(2)}) async-start(bf16[16,8,2048]{2,1,0:T(8,128)(2,1)} %shard_map.37), calls=%async_computation | async-start | bytes 1048576 | tf_op jit(solution)/shard_map/all_to_all | solution.py:138
  9.4 0.0 copy-done.1
  9.4 0.1 copy.4.pairs_any.pairs_v
  9.5 0.0 copy-start
  9.5 1.7 %fusion.window_ref = bf16[2048,128]{1,0:T(8,128)(2,1)S(1)} fusion(s32[2048]{0:T(1024)S(1)} %get-tuple-element.5, s32[2048]{0:T(1024)S(1)} %get-tuple-element.6, pred[2048]{0:T(1024)(128)(4,1)S(1)} %fusion.3), kind=kLoop, calls=%fused_computation.1 | loop fusion | flops 786432 | bytes 542720 | tf_op jit(solution)/shard_map/convert_element_type | solution.py:142
  11.2 12.4 %all-to-all-done.st_ref = bf16[16,8,2048]{2,1,0:T(8,128)(2,1)S(1)} async-done(((bf16[16,8,2048]{2,1,0:T(8,128)(2,1)}), bf16[16,8,2048]{2,1,0:T(8,128)(2,1)S(1)}, u32[]{:S(2)}, u32[]{:S(2)}) %all-to-all-start) | async-done | bytes 524320 | tf_op jit(solution)/shard_map/all_to_all | solution.py:138
  23.7 0.0 copy-done
  23.7 3.1 %shard_map.38 = f32[15,1,128]{2,1,0:T(1,128)} custom-call(s32[64,2]{1,0:T(8,128)S(1)} %copy.4.pairs_any.pairs_v, s32[64,2]{1,0:T(8,128)S(1)} %copy.4.pairs_any.pairs_v, bf16[16,8,2048]{2,1,0:T(8,128)(2,1)S(1)} %all-to-all-done.st_ref, bf16[15,64]{1,0:T(8,128)(2,1)S(1)} %copy-done, bf16[2048,128]{1,0:T(8,128)(2,1)S(1)} %fusion.window_ref), custom_call_target="tpu_custom_call" | custom-call | tf_op jit(solution)/shard_map/pallas_call | solution.py:143
  (2 shorter events, 0.0 us)
Async XLA Ops:
  2.0 7.4 %copy-start.1 = (s32[64,2]{0,1:T(2,128)S(1)}, s32[64,2]{0,1:T(2,128)}, u32[]{:S(2)}) copy-start(s32[64,2]{0,1:T(2,128)} %param.4) | copy-start | bytes 1540
  2.0 21.7 %all-to-all-start = ((bf16[16,8,2048]{2,1,0:T(8,128)(2,1)}), bf16[16,8,2048]{2,1,0:T(8,128)(2,1)S(1)}, u32[]{:S(2)}, u32[]{:S(2)}) async-start(bf16[16,8,2048]{2,1,0:T(8,128)(2,1)} %shard_map.37), calls=%async_computation | async-start | bytes 1048576 | tf_op jit(solution)/shard_map/all_to_all | solution.py:138
  9.5 14.1 %copy-start = (bf16[15,64]{1,0:T(8,128)(2,1)S(1)}, bf16[15,64]{1,0:T(8,128)(2,1)}, u32[]{:S(2)}) copy-start(bf16[15,64]{1,0:T(8,128)(2,1)} %inv_ref.1) | copy-start | bytes 5764

commit v18 on v17

--- a/solution.py
+++ b/solution.py
@@ -104,8 +104,8 @@
         out_ref[s] = series[s:s + 1, :]
 
 
-def regroup_kernel(in_hbm, out_ref, in_ref, sems):
-    n_chunk = out_ref.shape[0]
+def regroup_kernel(in_hbm, out_hbm, in_ref, sems, out_sems):
+    n_chunk = out_hbm.shape[0]
     half = n_chunk // 2
     rows_half = half * LOOK_R
     copies = []
@@ -115,11 +115,20 @@
             copy = pltpu.make_async_copy(in_hbm.at[k, rows], in_ref.at[k, rows], sems.at[2 * k + q])
             copy.start()
             copies.append(copy)
+    outs = []
     for k in range(2):
         for q in range(2):
             copies[2 * k + q].wait()
             for c in range(q * half, (q + 1) * half):
-                out_ref[c, k * LOOK_R:(k + 1) * LOOK_R, :] = in_ref[k, c * LOOK_R:(c + 1) * LOOK_R, :]
+                out = pltpu.make_async_copy(
+                    in_ref.at[k, pl.ds(c * LOOK_R, LOOK_R)],
+                    out_hbm.at[c, pl.ds(k * LOOK_R, LOOK_R)],
+                    out_sems.at[k * n_chunk + c],
+                )
+                out.start()
+                outs.append(out)
+    for out in outs:
+        out.wait()
 
 
 def per_device(slc, pairs, inverse):
@@ -132,8 +141,12 @@
         regroup_kernel,
         out_shape=jax.ShapeDtypeStruct((n_date, 2 * rows, cols), slc.dtype),
         in_specs=[pl.BlockSpec(memory_space=pl.ANY)],
-        out_specs=pl.BlockSpec(memory_space=pltpu.VMEM),
-        scratch_shapes=[pltpu.VMEM(slc.shape[1:], slc.dtype), pltpu.SemaphoreType.DMA((4,))],
+        out_specs=pl.BlockSpec(memory_space=pl.ANY),
+        scratch_shapes=[
+            pltpu.VMEM(slc.shape[1:], slc.dtype),
+            pltpu.SemaphoreType.DMA((4,)),
+            pltpu.SemaphoreType.DMA((2 * n_date,)),
+        ],
     )(slc[0])
     stripes = lax.all_to_all(chunks, "date", split_axis=0, concat_axis=0, tiled=True)
     assert rows == LOOK_R and n_date % 8 == 0 and n_pair % 8 == 0

time: 27.1 us -> 27.2 us (level)
  no operation moved by 1% of the time
where the time goes in v18:
time: 27.2 us; the launch traced here: 27 us
  waiting for transfers between devices  12.4 us (46%)
  starting transfers between devices  7.43 us (27%)
  Pallas kernels  5.23 us (19%)
  other arithmetic  1.71 us (6%)
    all_to_all x1, waiting for transfers between devices, per_device(): lax.all_to_all(chunks, 'date', split_axis=0, concat_axis=0, tiled=True)  12.4 us
    all_to_all x1, starting transfers between devices, per_device(): lax.all_to_all(chunks, 'date', split_axis=0, concat_axis=0, tiled=True)  7.43 us
    pallas_call x1, Pallas kernels, per_device(): pl.pallas_call(functools.partial(kernel, n_date, n_pair), out_shape=jax.S...  3.15 us
    pallas_call x1, Pallas kernels, per_device(): pl.pallas_call(regroup_kernel, out_shape=jax.ShapeDtypeStruct((n_date, 2...  2.08 us
    convert_element_type x1, other arithmetic, per_device(): (col == lax.broadcasted_iota(jnp.int32, (cols, looks), 1)).astype(jnp.bfl...  1.7 us
  transfers between devices with their start and end apart: 1, of which 1 were waited for; matrix products, arithmetic and copies ran while one was open for 7% of the time, Pallas kernels for 0%

profile of v18, /device:TPU:0, one launch (start us, length us, event | category | flops | bytes accessed | tf_op | source)
XLA Modules:
  0.0 27.0 jit_solution(1378392375636095791)
XLA Ops:
  0.0 2.1 %shard_map.37 = bf16[16,8,2048]{2,1,0:T(8,128)(2,1)} custom-call(bf16[2,64,2048]{2,1,0:T(8,128)(2,1)} %bitcast.1), custom_call_target="tpu_custom_call" | custom-call | tf_op jit(solution)/shard_map/pallas_call | solution.py:140
  2.1 0.0 copy-start.1
  2.1 7.4 %all-to-all-start = ((bf16[16,8,2048]{2,1,0:T(8,128)(2,1)}), bf16[16,8,2048]{2,1,0:T(8,128)(2,1)S(1)}, u32[]{:S(2)}, u32[]{:S(2)}) async-start(bf16[16,8,2048]{2,1,0:T(8,128)(2,1)} %shard_map.37), calls=%async_computation | async-start | bytes 1048576 | tf_op jit(solution)/shard_map/all_to_all | solution.py:151
  9.5 0.0 copy-done.1
  9.5 0.1 copy.4.pairs_any.pairs_v
  9.7 0.0 copy-start
  9.7 1.7 %fusion.window_ref = bf16[2048,128]{1,0:T(8,128)(2,1)S(1)} fusion(s32[2048]{0:T(1024)S(1)} %get-tuple-element.5, s32[2048]{0:T(1024)S(1)} %get-tuple-element.6, pred[2048]{0:T(1024)(128)(4,1)S(1)} %fusion.3), kind=kLoop, calls=%fused_computation.1 | loop fusion | flops 786432 | bytes 542720 | tf_op jit(solution)/shard_map/convert_element_type | solution.py:155
  11.4 12.4 %all-to-all-done.st_ref = bf16[16,8,2048]{2,1,0:T(8,128)(2,1)S(1)} async-done(((bf16[16,8,2048]{2,1,0:T(8,128)(2,1)}), bf16[16,8,2048]{2,1,0:T(8,128)(2,1)S(1)}, u32[]{:S(2)}, u32[]{:S(2)}) %all-to-all-start) | async-done | bytes 524320 | tf_op jit(solution)/shard_map/all_to_all | solution.py:151
  23.8 0.0 copy-done
  23.8 3.1 %shard_map.38 = f32[15,1,128]{2,1,0:T(1,128)} custom-call(s32[64,2]{1,0:T(8,128)S(1)} %copy.4.pairs_any.pairs_v, s32[64,2]{1,0:T(8,128)S(1)} %copy.4.pairs_any.pairs_v, bf16[16,8,2048]{2,1,0:T(8,128)(2,1)S(1)} %all-to-all-done.st_ref, bf16[15,64]{1,0:T(8,128)(2,1)S(1)} %copy-done, bf16[2048,128]{1,0:T(8,128)(2,1)S(1)} %fusion.window_ref), custom_call_target="tpu_custom_call" | custom-call | tf_op jit(solution)/shard_map/pallas_call | solution.py:156
  (2 shorter events, 0.0 us)
Async XLA Ops:
  2.1 7.4 %copy-start.1 = (s32[64,2]{0,1:T(2,128)S(1)}, s32[64,2]{0,1:T(2,128)}, u32[]{:S(2)}) copy-start(s32[64,2]{0,1:T(2,128)} %param.4) | copy-start | bytes 1540
  2.1 21.7 %all-to-all-start = ((bf16[16,8,2048]{2,1,0:T(8,128)(2,1)}), bf16[16,8,2048]{2,1,0:T(8,128)(2,1)S(1)}, u32[]{:S(2)}, u32[]{:S(2)}) async-start(bf16[16,8,2048]{2,1,0:T(8,128)(2,1)} %shard_map.37), calls=%async_computation | async-start | bytes 1048576 | tf_op jit(solution)/shard_map/all_to_all | solution.py:151
  9.7 14.1 %copy-start = (bf16[15,64]{1,0:T(8,128)(2,1)S(1)}, bf16[15,64]{1,0:T(8,128)(2,1)}, u32[]{:S(2)}) copy-start(bf16[15,64]{1,0:T(8,128)(2,1)} %inv_ref.1) | copy-start | bytes 5764

commit v19 on v17

--- a/solution.py
+++ b/solution.py
@@ -128,13 +128,14 @@
     steps = inverse.shape[0]
     _, _, all_rows, cols = slc.shape
     rows = all_rows // n_date
-    chunks = pl.pallas_call(
-        regroup_kernel,
-        out_shape=jax.ShapeDtypeStruct((n_date, 2 * rows, cols), slc.dtype),
-        in_specs=[pl.BlockSpec(memory_space=pl.ANY)],
-        out_specs=pl.BlockSpec(memory_space=pltpu.VMEM),
-        scratch_shapes=[pltpu.VMEM(slc.shape[1:], slc.dtype), pltpu.SemaphoreType.DMA((4,))],
-    )(slc[0])
+    size = 2 * all_rows
+    out_i = lax.broadcasted_iota(jnp.int32, (size, size), 0)
+    in_i = lax.broadcasted_iota(jnp.int32, (size, size), 1)
+    part = (out_i // rows) % 2
+    row = (out_i // (2 * rows)) * rows + out_i % rows
+    perm = ((in_i // all_rows == part) & (in_i % all_rows == row)).astype(slc.dtype)
+    flat = slc[0].reshape(size, cols)
+    chunks = jnp.dot(perm, flat, preferred_element_type=jnp.float32).astype(slc.dtype).reshape(n_date, 2 * rows, cols)
     stripes = lax.all_to_all(chunks, "date", split_axis=0, concat_axis=0, tiled=True)
     assert rows == LOOK_R and n_date % 8 == 0 and n_pair % 8 == 0
     looks = cols // LOOK_C

time: 27.1 us -> 27.6 us (1.018)
  Pallas kernels: 5.1 us -> 3.15 us
  matrix products: 0 us -> 1.26 us
  local copies, waits for them, and re-layouts: 0.11 us -> 1.07 us
    pallas_call x1 -> x0, Pallas kernels: 1.95 us -> none  [per_device(): pl.pallas_call(regroup_kernel, out_shape=jax.ShapeDtypeStruct((n_date, 2...]
    dot_general x0 -> x1, matrix products: none -> 1.26 us  [per_device(): jnp.dot(perm, flat, preferred_element_type=jnp.float32).astype(slc.dtype)]
    unnamed x5 -> x7, local copies, waits for them, and re-layouts: 0.11 us -> 1.07 us
where the time goes in v19:
time: 27.6 us; the launch traced here: 27.3 us
  waiting for transfers between devices  12.4 us (45%)
  starting transfers between devices  7.55 us (27%)
  Pallas kernels  3.15 us (11%)
  other arithmetic  1.76 us (6%)
  matrix products  1.26 us (5%)
  local copies, waits for them, and re-layouts  1.07 us (4%)
    all_to_all x1, waiting for transfers between devices, per_device(): lax.all_to_all(chunks, 'date', split_axis=0, concat_axis=0, tiled=True)  12.4 us
    all_to_all x1, starting transfers between devices, per_device(): lax.all_to_all(chunks, 'date', split_axis=0, concat_axis=0, tiled=True)  7.55 us
    pallas_call x1, Pallas kernels, per_device(): pl.pallas_call(functools.partial(kernel, n_date, n_pair), out_shape=jax.S...  3.15 us
    convert_element_type x1, other arithmetic, per_device(): (col == lax.broadcasted_iota(jnp.int32, (cols, looks), 1)).astype(jnp.bfl...  1.7 us
    dot_general x1, matrix products, per_device(): jnp.dot(perm, flat, preferred_element_type=jnp.float32).astype(slc.dtype)  1.26 us
    unnamed x7, local copies, waits for them, and re-layouts  1.07 us
  transfers between devices with their start and end apart: 1, of which 1 were waited for; matrix products, arithmetic and copies ran while one was open for 7% of the time, Pallas kernels for 0%

profile of v19, /device:TPU:0, one launch (start us, length us, event | category | flops | bytes accessed | tf_op | source)
XLA Modules:
  0.0 27.3 jit_solution(8847666948231521075)
XLA Ops:
  0.0 0.0 copy-start
  0.1 1.0 %copy-done = bf16[1,2,64,2048]{3,2,1,0:T(8,128)(2,1)S(1)} copy-done((bf16[1,2,64,2048]{3,2,1,0:T(8,128)(2,1)S(1)}, bf16[1,2,64,2048]{3,2,1,0:T(8,128)(2,1)}, u32[]{:S(2)}) %copy-start) | copy-done | bytes 524312
  1.0 1.3 %fusion = bf16[16,8,2048]{2,1,0:T(8,128)(2,1)} fusion(bf16[128,2048]{1,0:T(8,128)(2,1)S(1)} %bitcast.4, s32[128]{0:T(128)S(1)} %get-tuple-element.11, s32[128]{0:T(128)S(1)} %get-tuple-element.14, s32[128]{0:T(128)S(1)} %get-tuple-element.9, s32[128]{0:T(128)S(1)} %get-tuple-element.16, s32[128]{0:T(128)S(1)} %get-tuple-element.13, ...), kind=kOutput, calls=%fused_computation.1 | convolution fusion | flops 67715072 | bytes 1054336 | tf_op jit(solution)/shard_map/dot_general | solution.py:138
  2.3 0.0 copy-start.2
  2.3 7.5 %all-to-all-start = ((bf16[16,8,2048]{2,1,0:T(8,128)(2,1)}), bf16[16,8,2048]{2,1,0:T(8,128)(2,1)S(1)}, u32[]{:S(2)}, u32[]{:S(2)}) async-start(bf16[16,8,2048]{2,1,0:T(8,128)(2,1)} %fusion), calls=%async_computation | async-start | bytes 1048576 | tf_op jit(solution)/shard_map/all_to_all | solution.py:139
  9.9 0.0 copy-done.2
  9.9 0.1 copy.4.pairs_any.pairs_v
  10.0 0.0 copy-start.1
  10.0 1.7 %fusion.1.window_ref = bf16[2048,128]{1,0:T(8,128)(2,1)S(1)} fusion(s32[2048]{0:T(1024)S(1)} %get-tuple-element.19, s32[2048]{0:T(1024)S(1)} %get-tuple-element.20, pred[2048]{0:T(1024)(128)(4,1)S(1)} %fusion.31), kind=kLoop, calls=%fused_computation.3 | loop fusion | flops 786432 | bytes 542720 | tf_op jit(solution)/shard_map/convert_element_type | solution.py:143
  11.7 12.4 %all-to-all-done.st_ref = bf16[16,8,2048]{2,1,0:T(8,128)(2,1)S(1)} async-done(((bf16[16,8,2048]{2,1,0:T(8,128)(2,1)}), bf16[16,8,2048]{2,1,0:T(8,128)(2,1)S(1)}, u32[]{:S(2)}, u32[]{:S(2)}) %all-to-all-start) | async-done | bytes 524320 | tf_op jit(solution)/shard_map/all_to_all | solution.py:139
  24.1 0.0 copy-done.1
  24.1 3.1 %shard_map.37 = f32[15,1,128]{2,1,0:T(1,128)} custom-call(s32[64,2]{1,0:T(8,128)S(1)} %copy.4.pairs_any.pairs_v, s32[64,2]{1,0:T(8,128)S(1)} %copy.4.pairs_any.pairs_v, bf16[16,8,2048]{2,1,0:T(8,128)(2,1)S(1)} %all-to-all-done.st_ref, bf16[15,64]{1,0:T(8,128)(2,1)S(1)} %copy-done.1, bf16[2048,128]{1,0:T(8,128)(2,1)S(1)} %fusion.1.window_ref), custom_call_target="tpu_custom_call" | custom-call | tf_op jit(solution)/shard_map/pallas_call | solution.py:144
  (10 shorter events, 0.1 us)
Async XLA Ops:
  0.0 1.0 %copy-start = (bf16[1,2,64,2048]{3,2,1,0:T(8,128)(2,1)S(1)}, bf16[1,2,64,2048]{3,2,1,0:T(8,128)(2,1)}, u32[]{:S(2)}) copy-start(bf16[1,2,64,2048]{3,2,1,0:T(8,128)(2,1)} %param.3) | copy-start | bytes 1572868
  2.3 7.6 %copy-start.2 = (s32[64,2]{0,1:T(2,128)S(1)}, s32[64,2]{0,1:T(2,128)}, u32[]{:S(2)}) copy-start(s32[64,2]{0,1:T(2,128)} %param.4) | copy-start | bytes 1540
  2.3 21.8 %all-to-all-start = ((bf16[16,8,2048]{2,1,0:T(8,128)(2,1)}), bf16[16,8,2048]{2,1,0:T(8,128)(2,1)S(1)}, u32[]{:S(2)}, u32[]{:S(2)}) async-start(bf16[16,8,2048]{2,1,0:T(8,128)(2,1)} %fusion), calls=%async_computation | async-start | bytes 1048576 | tf_op jit(solution)/shard_map/all_to_all | solution.py:139
  10.0 14.1 %copy-start.1 = (bf16[15,64]{1,0:T(8,128)(2,1)S(1)}, bf16[15,64]{1,0:T(8,128)(2,1)}, u32[]{:S(2)}) copy-start(bf16[15,64]{1,0:T(8,128)(2,1)} %inv_ref.1) | copy-start | bytes 5764
